TPU v7x, 256 devices: a whole 4x4x8 slice. The times are simulated.
256 devices in a mesh: ctx: 16 (over y_lo, z), exp: 8 (over x, core), rep: 2 (over y_hi).
Axes of the slice: x: 4, y: 4 (y_hi: 2, y_lo: 2; y = y_hi * 2 + y_lo), z: 8, core: 2. Of those that a mesh axis runs over, the one named last changes fastest.
Arguments:
- sequence: bfloat16 [2, 2048, 2048], P('rep', 'ctx'), may hold values from -6 to 6
- norm1_gain: float32 [2048], replicated, may hold values from 0.1 to 1.9
- w_in: bfloat16 [2048, 3, 2048], P(None, None, 'exp'), may hold values from -0.125 to 0.125
- long_filter: float32 [2048, 2048], P('ctx', 'exp'), may hold values from -0.125 to 0.125
- filter_decay: float32 [2048], P('exp'), may hold values from 0.5 to 150
- conv_bias: float32 [2048], P('exp'), may hold values from -4 to 4
- w_out: bfloat16 [2048, 2048], P('exp'), may hold values from -0.125 to 0.125
- norm2_gain: float32 [2048], replicated, may hold values from 0.1 to 1.9
- router: bfloat16 [2048, 8], replicated, may hold values from -0.39648438 to 0.39648438
- w_gate: bfloat16 [8, 2048, 4096], P('exp', None, 'ctx'), may hold values from -0.125 to 0.125
- w_up: bfloat16 [8, 2048, 4096], P('exp', None, 'ctx'), may hold values from -0.125 to 0.125
- w_down: bfloat16 [8, 4096, 2048], P('exp', 'ctx'), may hold values from -0.09375 to 0.09375
- experts: int32 [2, 2048, 2], P('rep', ('ctx', 'exp')), may hold values from 0 to 7, as said below
- expert_slots: int32 [2, 2048, 2], P('rep', ('ctx', 'exp')), may hold values from 0 to 7, as said below
- splice_head: bfloat16 [112, 2048], replicated, may hold values from -0.125 to 0.125
- targets: float32 [2, 2048, 112], P('rep', ('ctx', 'exp')), may hold values from 0 to 1
Outputs:
- block_out: bfloat16 [2, 2048, 2048], P('rep', ('ctx', 'exp'))
- head_grad: float32 [112, 2048], replicated
Inputs may be any that keep to these rules, and one draw needn't show every extreme that they name: Each token names two different experts. Among the tokens of one aligned block of 16 tokens, no expert is named more than 8 times, and in each replica one expert is named exactly 8 times in every block. `expert_slots`: A choice's slot is the number of choices of the same expert before it within its aligned block of 16 tokens, in token order, a token's first choice before its second.
All inputs are finite; a program needn't handle non-finite values.
Results may differ from a plain program's by a relative error of at most 0.011.
Values may be sent and summed in bfloat16 or wider, within the bound.
No kernel may reach another device: no remote copies, remote signals or barrier semaphores. Data moves between devices by JAX's collectives and lax.ppermute only.
A program may use at most 64 MiB of HBM per device.

v0:
```python
import math

import jax
import jax.numpy as jnp
from jax import lax
from jax.sharding import PartitionSpec as P

TWO_PI = 2.0 * math.pi


def stored(values):
    return lax.optimization_barrier(values.astype(jnp.bfloat16))


def rms_scale(token_rows, norm_gain):
    wide = token_rows.astype(jnp.float32)
    inverse = lax.rsqrt(jnp.mean(wide * wide, axis=-1, keepdims=True) + 1e-05)
    return (wide * inverse * norm_gain).astype(jnp.bfloat16)


def phase_table(first_ids, second_ids, modulus):
    angle = (
        TWO_PI * (first_ids[:, None] * second_ids[None, :] % modulus).astype(jnp.float32) / modulus
    )
    return (jnp.cos(angle), jnp.sin(angle))


def spectra_move(blocks):
    return lax.all_to_all(blocks, "ctx", split_axis=0, concat_axis=1, tiled=True)


def a2a_reduce(values, axes, wire=None):
    count = lax.axis_size(axes)
    sent = values.reshape((count, -1) + values.shape[1:])
    if wire is not None:
        sent = sent.astype(wire)
    pieces = lax.all_to_all(sent, axes, 0, 0, tiled=True)
    return jnp.sum(pieces.astype(jnp.float32), axis=0)


def a2a_allreduce(values, axes, wire=None):
    count = lax.axis_size(axes)
    if values.shape[0] % count:
        return lax.psum(values, axes)
    mine = a2a_reduce(values, axes, wire)
    if wire is not None:
        mine = mine.astype(wire)
    spread = jnp.broadcast_to(mine[None], (count,) + mine.shape)
    gathered = lax.all_to_all(spread, axes, 0, 0, tiled=True)
    return gathered.astype(jnp.float32).reshape(values.shape)


def token_move(blocks):
    return lax.all_to_all(blocks, ("ctx", "exp"), split_axis=0, concat_axis=0, tiled=True)


def local_convolve(signal, kernel):
    highest = lax.Precision.HIGHEST
    lanes, length = signal.shape
    points = 2 * length
    outer = int(round(math.sqrt(points)))
    while points % outer:
        outer -= 1
    inner = points // outer
    half = length // inner
    rows = jnp.concatenate([signal, kernel], axis=0).reshape(2 * lanes, half, inner)
    a_ids = jnp.arange(half, dtype=jnp.int32)
    k1_ids = jnp.arange(outer, dtype=jnp.int32)
    b_ids = jnp.arange(inner, dtype=jnp.int32)
    k2_ids = jnp.arange(points // inner, dtype=jnp.int32)
    cos_first, sin_first = phase_table(a_ids, k1_ids, outer)
    cos_twist, sin_twist = phase_table(k1_ids, b_ids, points)
    cos_last, sin_last = phase_table(b_ids, k2_ids, inner)
    a_re = jnp.einsum("cab,ak->ckb", rows, cos_first, precision=highest)
    a_im = -jnp.einsum("cab,ak->ckb", rows, sin_first, precision=highest)
    b_re = a_re * cos_twist + a_im * sin_twist
    b_im = a_im * cos_twist - a_re * sin_twist
    x_re = jnp.einsum("ckb,bj->ckj", b_re, cos_last, precision=highest) + jnp.einsum(
        "ckb,bj->ckj", b_im, sin_last, precision=highest
    )
    x_im = jnp.einsum("ckb,bj->ckj", b_im, cos_last, precision=highest) - jnp.einsum(
        "ckb,bj->ckj", b_re, sin_last, precision=highest
    )
    p_re = x_re[:lanes] * x_re[lanes:] - x_im[:lanes] * x_im[lanes:]
    p_im = x_re[:lanes] * x_im[lanes:] + x_im[:lanes] * x_re[lanes:]
    c_re = jnp.einsum("ckj,mj->ckm", p_re, cos_last, precision=highest) - jnp.einsum(
        "ckj,mj->ckm", p_im, sin_last, precision=highest
    )
    c_im = jnp.einsum("ckj,mj->ckm", p_im, cos_last, precision=highest) + jnp.einsum(
        "ckj,mj->ckm", p_re, sin_last, precision=highest
    )
    d_re = c_re * cos_twist - c_im * sin_twist
    d_im = c_im * cos_twist + c_re * sin_twist
    out = jnp.einsum("ckm,lk->clm", d_re, cos_first, precision=highest) - jnp.einsum(
        "ckm,lk->clm", d_im, sin_first, precision=highest
    )
    return out.reshape(lanes, length) / points


def causal_convolve(source, shaped):
    both = jnp.stack([source.T, shaped.T], axis=0)
    whole = lax.all_to_all(both, "ctx", split_axis=1, concat_axis=2, tiled=True)
    convolved = local_convolve(whole[0], whole[1])
    back = lax.all_to_all(convolved, "ctx", split_axis=1, concat_axis=0, tiled=True)
    return back.T


def shards(
    sequence,
    norm1_gain,
    w_in,
    long_filter,
    filter_decay,
    conv_bias,
    w_out,
    norm2_gain,
    router,
    w_gate,
    w_up,
    w_down,
    experts,
    expert_slots,
    splice_head,
    targets,
):
    exp_count = lax.axis_size("exp")
    exp_pos = lax.axis_index("exp")
    ctx_count = lax.axis_size("ctx")
    ctx_pos = lax.axis_index("ctx")
    local_x = sequence[0]
    local_rows, model_width = local_x.shape
    own_rows = local_rows // exp_count
    length = local_rows * ctx_count
    normed = rms_scale(local_x, norm1_gain)
    projected = jnp.einsum("ti,igd->tgd", normed, w_in, preferred_element_type=jnp.float32)
    source = projected[:, 1] * projected[:, 0]
    positions = (ctx_pos * local_rows + jnp.arange(local_rows, dtype=jnp.int32)).astype(jnp.float32)
    shaped = long_filter * jnp.exp(-filter_decay[None, :] * positions[:, None] / length)
    convolved = causal_convolve(source, shaped)
    gated_rows = (projected[:, 2] * (convolved + conv_bias[None, :] * source)).astype(jnp.bfloat16)
    mixed_full = jnp.dot(gated_rows, w_out, preferred_element_type=jnp.float32)
    mixed_sum = a2a_reduce(mixed_full, "exp")
    residual_rows = lax.dynamic_slice_in_dim(local_x, exp_pos * own_rows, own_rows, 0)
    hidden_state = stored(residual_rows.astype(jnp.float32) + mixed_sum)
    routed_in = rms_scale(hidden_state, norm2_gain)
    chances = jax.nn.sigmoid(jnp.dot(routed_in, router, preferred_element_type=jnp.float32))
    picked_ids = experts[0]
    slot_ids = expert_slots[0]
    chosen = jnp.take_along_axis(chances, picked_ids, axis=1)
    weights = chosen / jnp.sum(chosen, axis=1, keepdims=True)
    n_experts = router.shape[1]
    capacity = 4 * own_rows // exp_count
    slot_rows = picked_ids * capacity + slot_ids
    buffer_ids = jnp.arange(n_experts * capacity, dtype=jnp.int32)[:, None]
    selector = (
        (slot_rows[None, :, 0] == buffer_ids) | (slot_rows[None, :, 1] == buffer_ids)
    ).astype(jnp.bfloat16)
    outgoing = jnp.dot(selector, routed_in, preferred_element_type=jnp.float32).astype(jnp.bfloat16)
    outgoing = outgoing.reshape(n_experts, capacity, model_width)
    gate_local = w_gate[0]
    up_local = w_up[0]
    down_local = w_down[0]
    copies = jnp.broadcast_to(outgoing[None], (ctx_count, n_experts, capacity, model_width))
    arrived = token_move(copies.reshape(ctx_count * n_experts, capacity, model_width))
    token_rows = arrived.reshape(-1, model_width)
    gate_val = jnp.dot(token_rows, gate_local, preferred_element_type=jnp.float32)
    up_val = jnp.dot(token_rows, up_local, preferred_element_type=jnp.float32)
    slice_hidden = (jax.nn.silu(gate_val) * up_val).astype(jnp.bfloat16)
    slice_part = (
        jnp.dot(slice_hidden, down_local, preferred_element_type=jnp.float32)
        .astype(jnp.bfloat16)
        .reshape(ctx_count * n_experts, capacity, model_width)
    )
    came_back = token_move(slice_part)
    summed = jnp.sum(
        came_back.reshape(ctx_count, n_experts, capacity, model_width).astype(jnp.float32), axis=0
    )
    expert_out = stored(summed)
    flat_out = expert_out.reshape(n_experts * capacity, model_width)
    first_rows = jnp.take(flat_out, slot_rows[:, 0], axis=0).astype(jnp.float32)
    second_rows = jnp.take(flat_out, slot_rows[:, 1], axis=0).astype(jnp.float32)
    combined = weights[:, 0:1] * first_rows + weights[:, 1:2] * second_rows
    block_final = stored(hidden_state.astype(jnp.float32) + combined)
    usage_prob = jax.nn.sigmoid(
        jnp.einsum("td,od->to", block_final, splice_head, preferred_element_type=jnp.float32)
    )
    all_tokens = lax.axis_size("rep") * ctx_count * exp_count * own_rows
    loss_scale = 1.0 / math.sqrt(all_tokens)
    usage_grad = ((usage_prob - targets[0]) * loss_scale).astype(jnp.bfloat16)
    local_grad = jnp.einsum(
        "td,to->do", block_final, usage_grad, preferred_element_type=jnp.float32
    )
    head_total = a2a_allreduce(local_grad, ("ctx", "exp", "rep"), jnp.bfloat16).T
    return (block_final[None], head_total)


def solution(mesh):
    in_specs = (
        P("rep", "ctx", None),
        P(),
        P(None, None, "exp"),
        P("ctx", "exp"),
        P("exp"),
        P("exp"),
        P("exp", None),
        P(),
        P(),
        P("exp", None, "ctx"),
        P("exp", None, "ctx"),
        P("exp", "ctx", None),
        P("rep", ("ctx", "exp"), None),
        P("rep", ("ctx", "exp"), None),
        P(),
        P("rep", ("ctx", "exp"), None),
    )
    out_specs = (P("rep", ("ctx", "exp"), None), P())
    return jax.shard_map(shards, mesh=mesh, in_specs=in_specs, out_specs=out_specs, check_vma=False)
```

profile of v0, /device:TPU:1, one launch (start us, length us, event | category | flops | bytes accessed | tf_op | source)
XLA Modules:
  0.0 377.7 jit_solution(5598025828378554344)
XLA Ops:
  0.7 1.4 fusion.22
  2.7 1.7 fusion.39
  6.2 10.1 %all-to-all-start = ((f32[2,256,128]{2,0,1:T(2,128)}), f32[2,256,128]{2,0,1:T(2,128)S(1)}, u32[]{:S(2)}, u32[]{:S(2)}) async-start(f32[2,256,128]{2,0,1:T(2,128)} %copy.32), calls=%async_computation | async-start | bytes 524288 | tf_op jit(solution)/shard_map/all_to_all | solution.py:102
  16.5 8.6 %all-to-all-done = f32[2,256,128]{2,0,1:T(2,128)S(1)} async-done(((f32[2,256,128]{2,0,1:T(2,128)}), f32[2,256,128]{2,0,1:T(2,128)S(1)}, u32[]{:S(2)}, u32[]{:S(2)}) %all-to-all-start) | async-done | bytes 262176 | tf_op jit(solution)/shard_map/all_to_all | solution.py:102
  28.2 1.6 copy.35
  31.6 2.1 fusion.96
  33.7 2.1 convolution_negate_fusion
  46.3 12.7 %all_to_all.56 = f32[16,16,128]{2,0,1:T(8,128)S(1)} all-to-all(f32[16,16,128]{2,0,1:T(8,128)S(1)} %copy.36), channel_id=1, replica_groups=mesh['ctx'=16,'exp'=8,'rep'=2] {'ctx'}, dimensions={1} | all-to-all | bytes 262144 | tf_op jit(solution)/shard_map/all_to_all | solution.py:104
  59.0 2.7 fusion.63
  61.7 6.8 %all-to-all-start.2 = ((f32[8,16,2048]{2,1,0:T(8,128)}), f32[8,16,2048]{2,1,0:T(8,128)}, u32[]{:S(2)}, u32[]{:S(2)}) async-start(f32[8,16,2048]{2,1,0:T(8,128)} %bitcast.172), calls=%async_computation.2 | async-start | bytes 2097152 | tf_op jit(solution)/shard_map/all_to_all | solution.py:37
  68.6 15.0 %all-to-all-done.2 = f32[8,16,2048]{2,1,0:T(8,128)} async-done(((f32[8,16,2048]{2,1,0:T(8,128)}), f32[8,16,2048]{2,1,0:T(8,128)}, u32[]{:S(2)}, u32[]{:S(2)}) %all-to-all-start.2) | async-done | bytes 1048608 | tf_op jit(solution)/shard_map/all_to_all | solution.py:37
  86.7 104.0 %all_to_all.57 = bf16[128,8,2048]{2,1,0:T(8,128)(2,1)S(1)} all-to-all(bf16[128,8,2048]{2,1,0:T(8,128)(2,1)S(1)} %bitcast.169), channel_id=1, replica_groups=mesh['ctx'=16,'exp'=8,'rep'=2] {'ctx','exp'}, dimensions={0} | all-to-all | bytes 8388608 | tf_op jit(solution)/shard_map/all_to_all | solution.py:54
  190.8 2.0 copy-done.1
  192.7 2.3 fusion.2
  195.1 9.4 %convert_bitcast_fusion = bf16[128,8,2048]{2,1,0:T(8,128)(2,1)} fusion(bf16[1,256,2048]{2,1,0:T(8,128)(2,1)} %param.29, bf16[128,8,2048]{2,1,0:T(8,128)(2,1)} %copy-done.1, bf16[1,2048,256]{2,1,0:T(8,128)(2,1)} %param.28, f32[1024,256]{1,0:T(8,128)} %fusion.2), kind=kOutput, calls=%fused_computation.7 | convolution fusion | flops 2151153664 | bytes 11534336 | tf_op jit(solution)/shard_map/dot_general | solution.py:170
  204.4 6.7 %all-to-all-start.4 = ((bf16[128,8,2048]{2,1,0:T(8,128)(2,1)}), bf16[128,8,2048]{2,1,0:T(8,128)(2,1)}, u32[]{:S(2)}, u32[]{:S(2)}) async-start(bf16[128,8,2048]{2,1,0:T(8,128)(2,1)} %convert_bitcast_fusion), calls=%async_computation.4 | async-start | bytes 8388608 | tf_op jit(solution)/shard_map/all_to_all | solution.py:54
  213.6 94.8 %all-to-all-done.4 = bf16[128,8,2048]{2,1,0:T(8,128)(2,1)} async-done(((bf16[128,8,2048]{2,1,0:T(8,128)(2,1)}), bf16[128,8,2048]{2,1,0:T(8,128)(2,1)}, u32[]{:S(2)}, u32[]{:S(2)}) %all-to-all-start.4) | async-done | bytes 4194336 | tf_op jit(solution)/shard_map/all_to_all | solution.py:54
  308.3 3.0 reduce_sum.64
  314.1 2.6 convolution_convert_fusion
  316.7 2.0 copy.40
  318.8 27.8 %all_to_all.58 = bf16[256,8,112]{2,1,0:T(8,128)(2,1)} all-to-all(bf16[256,8,112]{2,1,0:T(8,128)(2,1)} %bitcast.173), channel_id=1, replica_groups=mesh['ctx'=16,'exp'=8,'rep'=2] {'ctx','exp','rep'}, dimensions={0} | all-to-all | bytes 917504 | tf_op jit(solution)/shard_map/all_to_all | solution.py:37
  346.5 1.3 reduce_sum.65
  347.9 26.3 %all_to_all.59 = bf16[256,8,112]{2,1,0:T(8,128)(2,1)S(1)} all-to-all(bf16[256,8,112]{2,1,0:T(8,128)(2,1)S(1)} %broadcast_in_dim.21), channel_id=1, replica_groups=mesh['ctx'=16,'exp'=8,'rep'=2] {'ctx','exp','rep'}, dimensions={0} | all-to-all | bytes 917504 | tf_op jit(solution)/shard_map/all_to_all | solution.py:49
  375.2 2.5 copy.41
  (77 shorter events, 27.2 us)
Async XLA Ops:
  0.6 2.1 copy-start
  0.6 4.6 %copy-start.4 = (f32[128,256]{1,0:T(8,128)S(1)}, f32[128,256]{1,0:T(8,128)}, u32[]{:S(2)}) copy-start(f32[128,256]{1,0:T(8,128)} %param.21) | copy-start | bytes 393220
  4.4 0.8 copy-start.2
  6.2 18.9 %all-to-all-start = ((f32[2,256,128]{2,0,1:T(2,128)}), f32[2,256,128]{2,0,1:T(2,128)S(1)}, u32[]{:S(2)}, u32[]{:S(2)}) async-start(f32[2,256,128]{2,0,1:T(2,128)} %copy.32), calls=%async_computation | async-start | bytes 524288 | tf_op jit(solution)/shard_map/all_to_all | solution.py:102
  41.4 17.7 %copy-start.8 = (f32[256]{0:T(256)S(1)}, f32[256]{0:T(256)}, u32[]{:S(2)}) copy-start(f32[256]{0:T(256)} %param.23) | copy-start | bytes 3076
  43.5 25.1 %copy-start.5 = (s32[1,16,2]{1,2,0:T(2,128)S(1)}, s32[1,16,2]{1,2,0:T(2,128)}, u32[]{:S(2)}) copy-start(s32[1,16,2]{1,2,0:T(2,128)} %param.30) | copy-start | bytes 388
  43.5 25.1 %copy-start.9 = (s32[1,16,2]{1,2,0:T(2,128)S(1)}, s32[1,16,2]{1,2,0:T(2,128)}, u32[]{:S(2)}) copy-start(s32[1,16,2]{1,2,0:T(2,128)} %param.31) | copy-start | bytes 388
  44.0 41.9 %copy-start.7 = (f32[2048]{0:T(1024)S(1)}, f32[2048]{0:T(1024)}, u32[]{:S(2)}) copy-start(f32[2048]{0:T(1024)} %param.25) | copy-start | bytes 24580
  61.7 21.9 %all-to-all-start.2 = ((f32[8,16,2048]{2,1,0:T(8,128)}), f32[8,16,2048]{2,1,0:T(8,128)}, u32[]{:S(2)}, u32[]{:S(2)}) async-start(f32[8,16,2048]{2,1,0:T(8,128)} %bitcast.172), calls=%async_computation.2 | async-start | bytes 2097152 | tf_op jit(solution)/shard_map/all_to_all | solution.py:37
  86.7 106.0 %copy-start.10 = (bf16[1,2048,256]{2,1,0:T(8,128)(2,1)S(1)}, bf16[1,2048,256]{2,1,0:T(8,128)(2,1)}, u32[]{:S(2)}) copy-start(bf16[1,2048,256]{2,1,0:T(8,128)(2,1)} %param.27) | copy-start | bytes 3145732
  190.8 2.0 copy-start.1
  204.4 7.4 %copy-start.11 = (bf16[2048,8]{0,1:T(8,128)(2,1)S(1)}, bf16[2048,8]{0,1:T(8,128)(2,1)}, u32[]{:S(2)}) copy-start(bf16[2048,8]{0,1:T(8,128)(2,1)} %param.26) | copy-start | bytes 98308
  204.4 103.9 %all-to-all-start.4 = ((bf16[128,8,2048]{2,1,0:T(8,128)(2,1)}), bf16[128,8,2048]{2,1,0:T(8,128)(2,1)}, u32[]{:S(2)}, u32[]{:S(2)}) async-start(bf16[128,8,2048]{2,1,0:T(8,128)(2,1)} %convert_bitcast_fusion), calls=%async_computation.4 | async-start | bytes 8388608 | tf_op jit(solution)/shard_map/all_to_all | solution.py:54
  212.7 101.4 %copy-start.6 = (f32[1,16,112]{2,1,0:T(8,128)S(1)}, f32[1,16,112]{2,1,0:T(8,128)}, u32[]{:S(2)}) copy-start(f32[1,16,112]{2,1,0:T(8,128)} %param.33) | copy-start | bytes 21508
  314.1 63.6 %copy-start.3 = (bf16[16,2048]{1,0:T(8,128)(2,1)}, bf16[16,2048]{1,0:T(8,128)(2,1)S(1)}, u32[]{:S(2)}) copy-start(bf16[16,2048]{1,0:T(8,128)(2,1)S(1)} %fusion.59) | copy-start | bytes 196612
where the time goes:
time: 379 us; the launch traced here: 378 us
  blocking collectives  171 us (45%)
  waiting for transfers between devices  118 us (31%)
  matrix products  31.7 us (8%)
  starting transfers between devices  23.6 us (6%)
  local copies, waits for them, and re-layouts  20.4 us (5%)
  other arithmetic  11.8 us (3%)
    all_to_all x1, blocking collectives, token_move(): lax.all_to_all(blocks, ('ctx', 'exp'), split_axis=0, concat_axis=0, tiled...  104 us
    all_to_all x1, waiting for transfers between devices, token_move(): lax.all_to_all(blocks, ('ctx', 'exp'), split_axis=0, concat_axis=0, tiled...  94.8 us
    all_to_all x1, blocking collectives, a2a_reduce(): pieces = lax.all_to_all(sent, axes, 0, 0, tiled=True)  27.8 us
    all_to_all x1, blocking collectives, a2a_allreduce(): gathered = lax.all_to_all(spread, axes, 0, 0, tiled=True)  26.3 us
    all_to_all x1, waiting for transfers between devices, a2a_reduce(): pieces = lax.all_to_all(sent, axes, 0, 0, tiled=True)  15 us
    all_to_all x1, blocking collectives, causal_convolve(): lax.all_to_all(convolved, 'ctx', split_axis=1, concat_axis=0, tiled=True)  12.7 us
    all_to_all x1, starting transfers between devices, causal_convolve(): whole = lax.all_to_all(both, 'ctx', split_axis=1, concat_axis=2, tiled=True)  10.1 us
    dot_general x1, matrix products, shards(): jnp.dot(slice_hidden, down_local, preferred_element_type=jnp.float32)  9.37 us
  transfers between devices with their start and end apart: 3, of which 3 were waited for; matrix products, arithmetic and copies ran while one was open for 1% of the time, Pallas kernels for 0%

commit v1 on v0

--- a/solution.py
+++ b/solution.py
@@ -54,16 +54,16 @@
     return lax.all_to_all(blocks, ("ctx", "exp"), split_axis=0, concat_axis=0, tiled=True)
 
 
-def local_convolve(signal, kernel):
+def local_spectrum(rows):
     highest = lax.Precision.HIGHEST
-    lanes, length = signal.shape
+    lanes, length = rows.shape
     points = 2 * length
     outer = int(round(math.sqrt(points)))
     while points % outer:
         outer -= 1
     inner = points // outer
     half = length // inner
-    rows = jnp.concatenate([signal, kernel], axis=0).reshape(2 * lanes, half, inner)
+    rows = rows.reshape(lanes, half, inner)
     a_ids = jnp.arange(half, dtype=jnp.int32)
     k1_ids = jnp.arange(outer, dtype=jnp.int32)
     b_ids = jnp.arange(inner, dtype=jnp.int32)
@@ -81,8 +81,27 @@
     x_im = jnp.einsum("ckb,bj->ckj", b_im, cos_last, precision=highest) - jnp.einsum(
         "ckb,bj->ckj", b_re, sin_last, precision=highest
     )
-    p_re = x_re[:lanes] * x_re[lanes:] - x_im[:lanes] * x_im[lanes:]
-    p_im = x_re[:lanes] * x_im[lanes:] + x_im[:lanes] * x_re[lanes:]
+    return x_re, x_im
+
+
+def local_convolve(signal_re, signal_im, kernel_re, kernel_im, length):
+    highest = lax.Precision.HIGHEST
+    lanes = signal_re.shape[0]
+    points = 2 * length
+    outer = int(round(math.sqrt(points)))
+    while points % outer:
+        outer -= 1
+    inner = points // outer
+    half = length // inner
+    a_ids = jnp.arange(half, dtype=jnp.int32)
+    k1_ids = jnp.arange(outer, dtype=jnp.int32)
+    b_ids = jnp.arange(inner, dtype=jnp.int32)
+    k2_ids = jnp.arange(points // inner, dtype=jnp.int32)
+    cos_first, sin_first = phase_table(a_ids, k1_ids, outer)
+    cos_twist, sin_twist = phase_table(k1_ids, b_ids, points)
+    cos_last, sin_last = phase_table(b_ids, k2_ids, inner)
+    p_re = signal_re * kernel_re - signal_im * kernel_im
+    p_im = signal_re * kernel_im + signal_im * kernel_re
     c_re = jnp.einsum("ckj,mj->ckm", p_re, cos_last, precision=highest) - jnp.einsum(
         "ckj,mj->ckm", p_im, sin_last, precision=highest
     )
@@ -97,10 +116,14 @@
     return out.reshape(lanes, length) / points
 
 
-def causal_convolve(source, shaped):
-    both = jnp.stack([source.T, shaped.T], axis=0)
-    whole = lax.all_to_all(both, "ctx", split_axis=1, concat_axis=2, tiled=True)
-    convolved = local_convolve(whole[0], whole[1])
+def to_sequences(rows):
+    return lax.all_to_all(rows.T, "ctx", split_axis=0, concat_axis=1, tiled=True)
+
+
+def causal_convolve(source, kernel_re, kernel_im):
+    whole = to_sequences(source)
+    signal_re, signal_im = local_spectrum(whole)
+    convolved = local_convolve(signal_re, signal_im, kernel_re, kernel_im, whole.shape[1])
     back = lax.all_to_all(convolved, "ctx", split_axis=1, concat_axis=0, tiled=True)
     return back.T
 
@@ -131,15 +154,16 @@
     local_rows, model_width = local_x.shape
     own_rows = local_rows // exp_count
     length = local_rows * ctx_count
+    positions = (ctx_pos * local_rows + jnp.arange(local_rows, dtype=jnp.int32)).astype(jnp.float32)
+    shaped = long_filter * jnp.exp(-filter_decay[None, :] * positions[:, None] / length)
+    kernel_re, kernel_im = local_spectrum(to_sequences(shaped))
     normed = rms_scale(local_x, norm1_gain)
     projected = jnp.einsum("ti,igd->tgd", normed, w_in, preferred_element_type=jnp.float32)
     source = projected[:, 1] * projected[:, 0]
-    positions = (ctx_pos * local_rows + jnp.arange(local_rows, dtype=jnp.int32)).astype(jnp.float32)
-    shaped = long_filter * jnp.exp(-filter_decay[None, :] * positions[:, None] / length)
-    convolved = causal_convolve(source, shaped)
+    convolved = causal_convolve(source, kernel_re, kernel_im)
     gated_rows = (projected[:, 2] * (convolved + conv_bias[None, :] * source)).astype(jnp.bfloat16)
     mixed_full = jnp.dot(gated_rows, w_out, preferred_element_type=jnp.float32)
-    mixed_sum = a2a_reduce(mixed_full, "exp")
+    mixed_sum = a2a_reduce(mixed_full, "exp", jnp.bfloat16)
     residual_rows = lax.dynamic_slice_in_dim(local_x, exp_pos * own_rows, own_rows, 0)
     hidden_state = stored(residual_rows.astype(jnp.float32) + mixed_sum)
     routed_in = rms_scale(hidden_state, norm2_gain)

time: 379 us -> 378 us (level)
  waiting for transfers between devices: 118 us -> 110 us
  starting transfers between devices: 23.6 us -> 29.2 us
    all_to_all x1, waiting for transfers between devices: 15 us -> 9.42 us  [a2a_reduce(): pieces = lax.all_to_all(sent, axes, 0, 0, tiled=True)]
    all_to_all x1 -> x2, starting transfers between devices: 10.1 us -> 14.9 us  [to_sequences(): lax.all_to_all(rows.T, 'ctx', split_axis=0, concat_axis=1, tiled=True)]
    dot_general x6 -> x12, matrix products: 8.79 us -> 12.5 us  [the longest x2 2.62 us: local_spectrum(): jnp.einsum('ckb,bj->ckj', b_im, cos_last, precision=highest)]
    all_to_all x1 -> x2, waiting for transfers between devices: 8.63 us -> 5.62 us  [to_sequences(): lax.all_to_all(rows.T, 'ctx', split_axis=0, concat_axis=1, tiled=True)]
  transfers between devices with their start and end apart: 3 -> 4, of which waited for: 3 -> 4; matrix products, arithmetic and copies ran while one was open for 1% -> 3% of each run, Pallas kernels for 0% -> 0%
where the time goes in v1:
time: 378 us; the launch traced here: 377 us
  blocking collectives  170 us (45%)
  waiting for transfers between devices  110 us (29%)
  matrix products  35.3 us (9%)
  starting transfers between devices  29.2 us (8%)
  local copies, waits for them, and re-layouts  19.3 us (5%)
  other arithmetic  11.9 us (3%)
    all_to_all x1, blocking collectives, token_move(): lax.all_to_all(blocks, ('ctx', 'exp'), split_axis=0, concat_axis=0, tiled...  104 us
    all_to_all x1, waiting for transfers between devices, token_move(): lax.all_to_all(blocks, ('ctx', 'exp'), split_axis=0, concat_axis=0, tiled...  94.8 us
    all_to_all x1, blocking collectives, a2a_reduce(): pieces = lax.all_to_all(sent, axes, 0, 0, tiled=True)  27.8 us
    all_to_all x1, blocking collectives, a2a_allreduce(): gathered = lax.all_to_all(spread, axes, 0, 0, tiled=True)  26.3 us
    all_to_all x2, starting transfers between devices, to_sequences(): lax.all_to_all(rows.T, 'ctx', split_axis=0, concat_axis=1, tiled=True)  14.9 us
    all_to_all x1, blocking collectives, causal_convolve(): lax.all_to_all(convolved, 'ctx', split_axis=1, concat_axis=0, tiled=True)  12.2 us
    all_to_all x1, waiting for transfers between devices, a2a_reduce(): pieces = lax.all_to_all(sent, axes, 0, 0, tiled=True)  9.42 us
    dot_general x1, matrix products, shards(): jnp.dot(slice_hidden, down_local, preferred_element_type=jnp.float32)  9.38 us
  transfers between devices with their start and end apart: 4, of which 4 were waited for; matrix products, arithmetic and copies ran while one was open for 3% of the time, Pallas kernels for 0%

profile of v1, /device:TPU:1, one launch (start us, length us, event | category | flops | bytes accessed | tf_op | source)
XLA Modules:
  0.0 376.7 jit_solution(8639825438671476673)
XLA Ops:
  3.3 10.1 %all-to-all-start.1 = ((f32[16,16,128]{2,1,0:T(8,128)}), f32[16,16,128]{2,1,0:T(8,128)S(1)}, u32[]{:S(2)}, u32[]{:S(2)}) async-start(f32[16,16,128]{2,1,0:T(8,128)} %bitcast.16), calls=%async_computation.1 | async-start | bytes 262144 | tf_op jit(solution)/shard_map/all_to_all | solution.py:120
  14.6 1.7 fusion.33
  18.0 2.8 all-to-all-done.1
  20.8 4.8 %all-to-all-start = ((f32[16,16,128]{2,1,0:T(8,128)}), f32[16,16,128]{2,1,0:T(8,128)}, u32[]{:S(2)}, u32[]{:S(2)}) async-start(f32[16,16,128]{2,1,0:T(8,128)} %bitcast.8), calls=%async_computation | async-start | bytes 262144 | tf_op jit(solution)/shard_map/all_to_all | solution.py:120
  30.3 2.8 all-to-all-done
  33.1 1.6 copy.24
  37.2 1.9 fusion.35
  39.1 1.9 fusion.39
  51.0 12.2 %all_to_all.73 = f32[16,16,128]{2,0,1:T(8,128)S(1)} all-to-all(f32[16,16,128]{2,0,1:T(8,128)S(1)} %copy.27), channel_id=1, replica_groups=mesh['ctx'=16,'exp'=8,'rep'=2] {'ctx'}, dimensions={1} | all-to-all | bytes 262144 | tf_op jit(solution)/shard_map/all_to_all | solution.py:127
  63.3 2.5 convolution_convert_fusion
  65.9 7.6 %all-to-all-start.3 = ((bf16[8,16,2048]{2,1,0:T(8,128)(2,1)}), bf16[8,16,2048]{2,1,0:T(8,128)(2,1)}, u32[]{:S(2)}, u32[]{:S(2)}) async-start(bf16[8,16,2048]{2,1,0:T(8,128)(2,1)} %bitcast.193), calls=%async_computation.3 | async-start | bytes 1048576 | tf_op jit(solution)/shard_map/all_to_all | solution.py:37
  73.5 9.4 %all-to-all-done.3 = bf16[8,16,2048]{2,1,0:T(8,128)(2,1)} async-done(((bf16[8,16,2048]{2,1,0:T(8,128)(2,1)}), bf16[8,16,2048]{2,1,0:T(8,128)(2,1)}, u32[]{:S(2)}, u32[]{:S(2)}) %all-to-all-start.3) | async-done | bytes 524320 | tf_op jit(solution)/shard_map/all_to_all | solution.py:37
  85.9 103.9 %all_to_all.74 = bf16[128,8,2048]{2,1,0:T(8,128)(2,1)S(1)} all-to-all(bf16[128,8,2048]{2,1,0:T(8,128)(2,1)S(1)} %bitcast.190), channel_id=1, replica_groups=mesh['ctx'=16,'exp'=8,'rep'=2] {'ctx','exp'}, dimensions={0} | all-to-all | bytes 8388608 | tf_op jit(solution)/shard_map/all_to_all | solution.py:54
  189.7 2.0 copy-done.3
  191.7 2.3 fusion.2
  194.0 9.4 %convert_bitcast_fusion = bf16[128,8,2048]{2,1,0:T(8,128)(2,1)} fusion(bf16[1,256,2048]{2,1,0:T(8,128)(2,1)} %param.29, bf16[128,8,2048]{2,1,0:T(8,128)(2,1)} %copy-done.3, bf16[1,2048,256]{2,1,0:T(8,128)(2,1)} %param.28, f32[1024,256]{1,0:T(8,128)} %fusion.2), kind=kOutput, calls=%fused_computation.7 | convolution fusion | flops 2151153664 | bytes 11534336 | tf_op jit(solution)/shard_map/dot_general | solution.py:194
  203.4 6.7 %all-to-all-start.5 = ((bf16[128,8,2048]{2,1,0:T(8,128)(2,1)}), bf16[128,8,2048]{2,1,0:T(8,128)(2,1)}, u32[]{:S(2)}, u32[]{:S(2)}) async-start(bf16[128,8,2048]{2,1,0:T(8,128)(2,1)} %convert_bitcast_fusion), calls=%async_computation.5 | async-start | bytes 8388608 | tf_op jit(solution)/shard_map/all_to_all | solution.py:54
  212.6 94.8 %all-to-all-done.5 = bf16[128,8,2048]{2,1,0:T(8,128)(2,1)} async-done(((bf16[128,8,2048]{2,1,0:T(8,128)(2,1)}), bf16[128,8,2048]{2,1,0:T(8,128)(2,1)}, u32[]{:S(2)}, u32[]{:S(2)}) %all-to-all-start.5) | async-done | bytes 4194336 | tf_op jit(solution)/shard_map/all_to_all | solution.py:54
  307.3 3.0 reduce_sum.64
  313.1 2.6 convolution_convert_fusion.1
  315.7 2.0 copy.31
  317.7 27.8 %all_to_all.75 = bf16[256,8,112]{2,1,0:T(8,128)(2,1)} all-to-all(bf16[256,8,112]{2,1,0:T(8,128)(2,1)} %bitcast.194), channel_id=1, replica_groups=mesh['ctx'=16,'exp'=8,'rep'=2] {'ctx','exp','rep'}, dimensions={0} | all-to-all | bytes 917504 | tf_op jit(solution)/shard_map/all_to_all | solution.py:37
  346.9 26.3 %all_to_all.76 = bf16[256,8,112]{2,1,0:T(8,128)(2,1)S(1)} all-to-all(bf16[256,8,112]{2,1,0:T(8,128)(2,1)S(1)} %broadcast_in_dim.21), channel_id=1, replica_groups=mesh['ctx'=16,'exp'=8,'rep'=2] {'ctx','exp','rep'}, dimensions={0} | all-to-all | bytes 917504 | tf_op jit(solution)/shard_map/all_to_all | solution.py:49
  374.2 2.5 copy.32
  (82 shorter events, 33.2 us)
Async XLA Ops:
  0.6 14.0 %copy-start = (bf16[2048,3,256]{2,0,1:T(8,128)(2,1)S(1)}, bf16[2048,3,256]{2,0,1:T(8,128)(2,1)}, u32[]{:S(2)}) copy-start(bf16[2048,3,256]{2,0,1:T(8,128)(2,1)} %param.20) | copy-start | bytes 9437188
  3.3 17.6 %all-to-all-start.1 = ((f32[16,16,128]{2,1,0:T(8,128)}), f32[16,16,128]{2,1,0:T(8,128)S(1)}, u32[]{:S(2)}, u32[]{:S(2)}) async-start(f32[16,16,128]{2,1,0:T(8,128)} %bitcast.16), calls=%async_computation.1 | async-start | bytes 262144 | tf_op jit(solution)/shard_map/all_to_all | solution.py:120
  16.3 0.7 copy-start.4
  20.8 12.3 %all-to-all-start = ((f32[16,16,128]{2,1,0:T(8,128)}), f32[16,16,128]{2,1,0:T(8,128)}, u32[]{:S(2)}, u32[]{:S(2)}) async-start(f32[16,16,128]{2,1,0:T(8,128)} %bitcast.8), calls=%async_computation | async-start | bytes 262144 | tf_op jit(solution)/shard_map/all_to_all | solution.py:120
  35.7 6.7 %copy-start.1 = (f32[64,16,64]{2,0,1:T(8,128)S(1)}, f32[64,16,64]{2,0,1:T(8,128)}, u32[]{:S(2)}) copy-start(f32[64,16,64]{2,0,1:T(8,128)} %fusion.106) | copy-start | bytes 786436
  35.7 6.7 %copy-start.2 = (f32[64,16,64]{2,0,1:T(8,128)S(1)}, f32[64,16,64]{2,0,1:T(8,128)}, u32[]{:S(2)}) copy-start(f32[64,16,64]{2,0,1:T(8,128)} %convolution_negate_fusion) | copy-start | bytes 786436
  46.1 17.2 %copy-start.9 = (f32[256]{0:T(256)S(1)}, f32[256]{0:T(256)}, u32[]{:S(2)}) copy-start(f32[256]{0:T(256)} %param.23) | copy-start | bytes 3076
  47.5 26.0 %copy-start.6 = (s32[1,16,2]{1,2,0:T(2,128)S(1)}, s32[1,16,2]{1,2,0:T(2,128)}, u32[]{:S(2)}) copy-start(s32[1,16,2]{1,2,0:T(2,128)} %param.30) | copy-start | bytes 388
  47.5 26.0 %copy-start.10 = (s32[1,16,2]{1,2,0:T(2,128)S(1)}, s32[1,16,2]{1,2,0:T(2,128)}, u32[]{:S(2)}) copy-start(s32[1,16,2]{1,2,0:T(2,128)} %param.31) | copy-start | bytes 388
  48.2 36.8 %copy-start.8 = (f32[2048]{0:T(1024)S(1)}, f32[2048]{0:T(1024)}, u32[]{:S(2)}) copy-start(f32[2048]{0:T(1024)} %param.25) | copy-start | bytes 24580
  65.9 17.1 %all-to-all-start.3 = ((bf16[8,16,2048]{2,1,0:T(8,128)(2,1)}), bf16[8,16,2048]{2,1,0:T(8,128)(2,1)}, u32[]{:S(2)}, u32[]{:S(2)}) async-start(bf16[8,16,2048]{2,1,0:T(8,128)(2,1)} %bitcast.193), calls=%async_computation.3 | async-start | bytes 1048576 | tf_op jit(solution)/shard_map/all_to_all | solution.py:37
  85.9 105.8 %copy-start.11 = (bf16[1,2048,256]{2,1,0:T(8,128)(2,1)S(1)}, bf16[1,2048,256]{2,1,0:T(8,128)(2,1)}, u32[]{:S(2)}) copy-start(bf16[1,2048,256]{2,1,0:T(8,128)(2,1)} %param.27) | copy-start | bytes 3145732
  189.7 2.0 copy-start.3
  203.4 7.4 %copy-start.12 = (bf16[2048,8]{0,1:T(8,128)(2,1)S(1)}, bf16[2048,8]{0,1:T(8,128)(2,1)}, u32[]{:S(2)}) copy-start(bf16[2048,8]{0,1:T(8,128)(2,1)} %param.26) | copy-start | bytes 98308
  203.4 103.9 %all-to-all-start.5 = ((bf16[128,8,2048]{2,1,0:T(8,128)(2,1)}), bf16[128,8,2048]{2,1,0:T(8,128)(2,1)}, u32[]{:S(2)}, u32[]{:S(2)}) async-start(bf16[128,8,2048]{2,1,0:T(8,128)(2,1)} %convert_bitcast_fusion), calls=%async_computation.5 | async-start | bytes 8388608 | tf_op jit(solution)/shard_map/all_to_all | solution.py:54
  211.8 101.4 %copy-start.7 = (f32[1,16,112]{2,1,0:T(8,128)S(1)}, f32[1,16,112]{2,1,0:T(8,128)}, u32[]{:S(2)}) copy-start(f32[1,16,112]{2,1,0:T(8,128)} %param.33) | copy-start | bytes 21508
  313.1 63.6 %copy-start.5 = (bf16[16,2048]{1,0:T(8,128)(2,1)}, bf16[16,2048]{1,0:T(8,128)(2,1)S(1)}, u32[]{:S(2)}) copy-start(bf16[16,2048]{1,0:T(8,128)(2,1)S(1)} %fusion.65) | copy-start | bytes 196612

commit v2 on v0

--- a/solution.py
+++ b/solution.py
@@ -139,7 +139,7 @@
     convolved = causal_convolve(source, shaped)
     gated_rows = (projected[:, 2] * (convolved + conv_bias[None, :] * source)).astype(jnp.bfloat16)
     mixed_full = jnp.dot(gated_rows, w_out, preferred_element_type=jnp.float32)
-    mixed_sum = a2a_reduce(mixed_full, "exp")
+    mixed_sum = a2a_reduce(mixed_full, "exp", jnp.bfloat16)
     residual_rows = lax.dynamic_slice_in_dim(local_x, exp_pos * own_rows, own_rows, 0)
     hidden_state = stored(residual_rows.astype(jnp.float32) + mixed_sum)
     routed_in = rms_scale(hidden_state, norm2_gain)
@@ -165,7 +165,7 @@
     token_rows = arrived.reshape(-1, model_width)
     gate_val = jnp.dot(token_rows, gate_local, preferred_element_type=jnp.float32)
     up_val = jnp.dot(token_rows, up_local, preferred_element_type=jnp.float32)
-    slice_hidden = (jax.nn.silu(gate_val) * up_val).astype(jnp.bfloat16)
+    slice_hidden = lax.optimization_barrier((jax.nn.silu(gate_val) * up_val).astype(jnp.bfloat16))
     slice_part = (
         jnp.dot(slice_hidden, down_local, preferred_element_type=jnp.float32)
         .astype(jnp.bfloat16)

time: 379 us -> 365 us (0.963)
  matrix products: 31.7 us -> 25.6 us
  waiting for transfers between devices: 118 us -> 113 us
    dot_general x1, matrix products: 9.37 us -> 3.24 us  [shards(): jnp.dot(slice_hidden, down_local, preferred_element_type=jnp.float32)]
    all_to_all x1, waiting for transfers between devices: 15 us -> 9.42 us  [a2a_reduce(): pieces = lax.all_to_all(sent, axes, 0, 0, tiled=True)]
where the time goes in v2:
time: 365 us; the launch traced here: 364 us
  blocking collectives  171 us (47%)
  waiting for transfers between devices  113 us (31%)
  matrix products  25.6 us (7%)
  starting transfers between devices  23.6 us (6%)
  local copies, waits for them, and re-layouts  18.4 us (5%)
  other arithmetic  11.7 us (3%)
    all_to_all x1, blocking collectives, token_move(): lax.all_to_all(blocks, ('ctx', 'exp'), split_axis=0, concat_axis=0, tiled...  104 us
    all_to_all x1, waiting for transfers between devices, token_move(): lax.all_to_all(blocks, ('ctx', 'exp'), split_axis=0, concat_axis=0, tiled...  94.8 us
    all_to_all x1, blocking collectives, a2a_reduce(): pieces = lax.all_to_all(sent, axes, 0, 0, tiled=True)  27.8 us
    all_to_all x1, blocking collectives, a2a_allreduce(): gathered = lax.all_to_all(spread, axes, 0, 0, tiled=True)  26.3 us
    all_to_all x1, blocking collectives, causal_convolve(): lax.all_to_all(convolved, 'ctx', split_axis=1, concat_axis=0, tiled=True)  12.7 us
    all_to_all x1, starting transfers between devices, causal_convolve(): whole = lax.all_to_all(both, 'ctx', split_axis=1, concat_axis=2, tiled=True)  10.1 us
    all_to_all x1, waiting for transfers between devices, a2a_reduce(): pieces = lax.all_to_all(sent, axes, 0, 0, tiled=True)  9.42 us
    all_to_all x1, waiting for transfers between devices, causal_convolve(): whole = lax.all_to_all(both, 'ctx', split_axis=1, concat_axis=2, tiled=True)  8.63 us
  transfers between devices with their start and end apart: 3, of which 3 were waited for; matrix products, arithmetic and copies ran while one was open for 1% of the time, Pallas kernels for 0%

profile of v2, /device:TPU:1, one launch (start us, length us, event | category | flops | bytes accessed | tf_op | source)
XLA Modules:
  0.0 363.9 jit_solution(1200865286625578611)
XLA Ops:
  0.7 1.4 fusion.22
  2.7 1.7 fusion.35
  6.2 10.1 %all-to-all-start = ((f32[2,256,128]{2,0,1:T(2,128)}), f32[2,256,128]{2,0,1:T(2,128)S(1)}, u32[]{:S(2)}, u32[]{:S(2)}) async-start(f32[2,256,128]{2,0,1:T(2,128)} %copy.32), calls=%async_computation | async-start | bytes 524288 | tf_op jit(solution)/shard_map/all_to_all | solution.py:102
  16.4 8.6 %all-to-all-done = f32[2,256,128]{2,0,1:T(2,128)S(1)} async-done(((f32[2,256,128]{2,0,1:T(2,128)}), f32[2,256,128]{2,0,1:T(2,128)S(1)}, u32[]{:S(2)}, u32[]{:S(2)}) %all-to-all-start) | async-done | bytes 262176 | tf_op jit(solution)/shard_map/all_to_all | solution.py:102
  28.2 1.6 copy.35
  31.5 2.1 fusion.90
  33.7 2.1 convolution_negate_fusion
  46.2 12.7 %all_to_all.56 = f32[16,16,128]{2,0,1:T(8,128)S(1)} all-to-all(f32[16,16,128]{2,0,1:T(8,128)S(1)} %copy.36), channel_id=1, replica_groups=mesh['ctx'=16,'exp'=8,'rep'=2] {'ctx'}, dimensions={1} | all-to-all | bytes 262144 | tf_op jit(solution)/shard_map/all_to_all | solution.py:104
  59.0 2.5 convolution_convert_fusion
  61.5 6.8 %all-to-all-start.2 = ((bf16[8,16,2048]{2,1,0:T(8,128)(2,1)}), bf16[8,16,2048]{2,1,0:T(8,128)(2,1)}, u32[]{:S(2)}, u32[]{:S(2)}) async-start(bf16[8,16,2048]{2,1,0:T(8,128)(2,1)} %bitcast.169), calls=%async_computation.2 | async-start | bytes 1048576 | tf_op jit(solution)/shard_map/all_to_all | solution.py:37
  68.4 9.4 %all-to-all-done.2 = bf16[8,16,2048]{2,1,0:T(8,128)(2,1)} async-done(((bf16[8,16,2048]{2,1,0:T(8,128)(2,1)}), bf16[8,16,2048]{2,1,0:T(8,128)(2,1)}, u32[]{:S(2)}, u32[]{:S(2)}) %all-to-all-start.2) | async-done | bytes 524320 | tf_op jit(solution)/shard_map/all_to_all | solution.py:37
  80.7 104.0 %all_to_all.57 = bf16[128,8,2048]{2,1,0:T(8,128)(2,1)S(1)} all-to-all(bf16[128,8,2048]{2,1,0:T(8,128)(2,1)S(1)} %bitcast.166), channel_id=1, replica_groups=mesh['ctx'=16,'exp'=8,'rep'=2] {'ctx','exp'}, dimensions={0} | all-to-all | bytes 8388608 | tf_op jit(solution)/shard_map/all_to_all | solution.py:54
  184.8 1.3 fusion.2
  186.1 1.3 fusion.8
  187.3 3.2 convert_bitcast_fusion
  190.6 6.6 %all-to-all-start.4 = ((bf16[128,8,2048]{2,1,0:T(8,128)(2,1)}), bf16[128,8,2048]{2,1,0:T(8,128)(2,1)}, u32[]{:S(2)}, u32[]{:S(2)}) async-start(bf16[128,8,2048]{2,1,0:T(8,128)(2,1)} %convert_bitcast_fusion), calls=%async_computation.4 | async-start | bytes 8388608 | tf_op jit(solution)/shard_map/all_to_all | solution.py:54
  199.7 94.8 %all-to-all-done.4 = bf16[128,8,2048]{2,1,0:T(8,128)(2,1)} async-done(((bf16[128,8,2048]{2,1,0:T(8,128)(2,1)}), bf16[128,8,2048]{2,1,0:T(8,128)(2,1)}, u32[]{:S(2)}, u32[]{:S(2)}) %all-to-all-start.4) | async-done | bytes 4194336 | tf_op jit(solution)/shard_map/all_to_all | solution.py:54
  294.5 3.0 reduce_sum.64
  300.3 2.6 convolution_convert_fusion.1
  302.9 2.0 copy.40
  304.9 27.8 %all_to_all.58 = bf16[256,8,112]{2,1,0:T(8,128)(2,1)} all-to-all(bf16[256,8,112]{2,1,0:T(8,128)(2,1)} %bitcast.170), channel_id=1, replica_groups=mesh['ctx'=16,'exp'=8,'rep'=2] {'ctx','exp','rep'}, dimensions={0} | all-to-all | bytes 917504 | tf_op jit(solution)/shard_map/all_to_all | solution.py:37
  332.7 1.3 reduce_sum.65
  334.1 26.3 %all_to_all.59 = bf16[256,8,112]{2,1,0:T(8,128)(2,1)S(1)} all-to-all(bf16[256,8,112]{2,1,0:T(8,128)(2,1)S(1)} %broadcast_in_dim.21), channel_id=1, replica_groups=mesh['ctx'=16,'exp'=8,'rep'=2] {'ctx','exp','rep'}, dimensions={0} | all-to-all | bytes 917504 | tf_op jit(solution)/shard_map/all_to_all | solution.py:49
  361.4 2.5 copy.41
  (80 shorter events, 27.1 us)
Async XLA Ops:
  0.6 2.1 copy-start
  0.6 4.5 %copy-start.4 = (f32[128,256]{1,0:T(8,128)S(1)}, f32[128,256]{1,0:T(8,128)}, u32[]{:S(2)}) copy-start(f32[128,256]{1,0:T(8,128)} %param.21) | copy-start | bytes 393220
  4.4 0.7 copy-start.1
  6.2 18.9 %all-to-all-start = ((f32[2,256,128]{2,0,1:T(2,128)}), f32[2,256,128]{2,0,1:T(2,128)S(1)}, u32[]{:S(2)}, u32[]{:S(2)}) async-start(f32[2,256,128]{2,0,1:T(2,128)} %copy.32), calls=%async_computation | async-start | bytes 524288 | tf_op jit(solution)/shard_map/all_to_all | solution.py:102
  41.3 17.7 %copy-start.8 = (f32[256]{0:T(256)S(1)}, f32[256]{0:T(256)}, u32[]{:S(2)}) copy-start(f32[256]{0:T(256)} %param.23) | copy-start | bytes 3076
  42.7 25.6 %copy-start.5 = (s32[1,16,2]{1,2,0:T(2,128)S(1)}, s32[1,16,2]{1,2,0:T(2,128)}, u32[]{:S(2)}) copy-start(s32[1,16,2]{1,2,0:T(2,128)} %param.30) | copy-start | bytes 388
  42.7 25.6 %copy-start.9 = (s32[1,16,2]{1,2,0:T(2,128)S(1)}, s32[1,16,2]{1,2,0:T(2,128)}, u32[]{:S(2)}) copy-start(s32[1,16,2]{1,2,0:T(2,128)} %param.31) | copy-start | bytes 388
  43.5 36.5 %copy-start.7 = (f32[2048]{0:T(1024)S(1)}, f32[2048]{0:T(1024)}, u32[]{:S(2)}) copy-start(f32[2048]{0:T(1024)} %param.25) | copy-start | bytes 24580
  61.5 16.3 %all-to-all-start.2 = ((bf16[8,16,2048]{2,1,0:T(8,128)(2,1)}), bf16[8,16,2048]{2,1,0:T(8,128)(2,1)}, u32[]{:S(2)}, u32[]{:S(2)}) async-start(bf16[8,16,2048]{2,1,0:T(8,128)(2,1)} %bitcast.169), calls=%async_computation.2 | async-start | bytes 1048576 | tf_op jit(solution)/shard_map/all_to_all | solution.py:37
  80.7 104.0 %copy-start.10 = (bf16[1,2048,256]{2,1,0:T(8,128)(2,1)S(1)}, bf16[1,2048,256]{2,1,0:T(8,128)(2,1)}, u32[]{:S(2)}) copy-start(bf16[1,2048,256]{2,1,0:T(8,128)(2,1)} %param.27) | copy-start | bytes 3145732
  184.8 1.3 copy-start.11
  186.0 1.3 copy-start.2
  190.6 7.4 %copy-start.12 = (bf16[2048,8]{0,1:T(8,128)(2,1)S(1)}, bf16[2048,8]{0,1:T(8,128)(2,1)}, u32[]{:S(2)}) copy-start(bf16[2048,8]{0,1:T(8,128)(2,1)} %param.26) | copy-start | bytes 98308
  190.6 103.9 %all-to-all-start.4 = ((bf16[128,8,2048]{2,1,0:T(8,128)(2,1)}), bf16[128,8,2048]{2,1,0:T(8,128)(2,1)}, u32[]{:S(2)}, u32[]{:S(2)}) async-start(bf16[128,8,2048]{2,1,0:T(8,128)(2,1)} %convert_bitcast_fusion), calls=%async_computation.4 | async-start | bytes 8388608 | tf_op jit(solution)/shard_map/all_to_all | solution.py:54
  198.9 101.4 %copy-start.6 = (f32[1,16,112]{2,1,0:T(8,128)S(1)}, f32[1,16,112]{2,1,0:T(8,128)}, u32[]{:S(2)}) copy-start(f32[1,16,112]{2,1,0:T(8,128)} %param.33) | copy-start | bytes 21508
  300.3 63.6 %copy-start.3 = (bf16[16,2048]{1,0:T(8,128)(2,1)}, bf16[16,2048]{1,0:T(8,128)(2,1)S(1)}, u32[]{:S(2)}) copy-start(bf16[16,2048]{1,0:T(8,128)(2,1)S(1)} %fusion.54) | copy-start | bytes 196612

commit v3 on v2

--- a/solution.py
+++ b/solution.py
@@ -71,29 +71,40 @@
     cos_first, sin_first = phase_table(a_ids, k1_ids, outer)
     cos_twist, sin_twist = phase_table(k1_ids, b_ids, points)
     cos_last, sin_last = phase_table(b_ids, k2_ids, inner)
-    a_re = jnp.einsum("cab,ak->ckb", rows, cos_first, precision=highest)
-    a_im = -jnp.einsum("cab,ak->ckb", rows, sin_first, precision=highest)
-    b_re = a_re * cos_twist + a_im * sin_twist
-    b_im = a_im * cos_twist - a_re * sin_twist
-    x_re = jnp.einsum("ckb,bj->ckj", b_re, cos_last, precision=highest) + jnp.einsum(
-        "ckb,bj->ckj", b_im, sin_last, precision=highest
-    )
-    x_im = jnp.einsum("ckb,bj->ckj", b_im, cos_last, precision=highest) - jnp.einsum(
-        "ckb,bj->ckj", b_re, sin_last, precision=highest
-    )
-    p_re = x_re[:lanes] * x_re[lanes:] - x_im[:lanes] * x_im[lanes:]
-    p_im = x_re[:lanes] * x_im[lanes:] + x_im[:lanes] * x_re[lanes:]
-    c_re = jnp.einsum("ckj,mj->ckm", p_re, cos_last, precision=highest) - jnp.einsum(
-        "ckj,mj->ckm", p_im, sin_last, precision=highest
-    )
-    c_im = jnp.einsum("ckj,mj->ckm", p_im, cos_last, precision=highest) + jnp.einsum(
-        "ckj,mj->ckm", p_re, sin_last, precision=highest
-    )
-    d_re = c_re * cos_twist - c_im * sin_twist
-    d_im = c_im * cos_twist + c_re * sin_twist
-    out = jnp.einsum("ckm,lk->clm", d_re, cos_first, precision=highest) - jnp.einsum(
-        "ckm,lk->clm", d_im, sin_first, precision=highest
-    )
+    first = jnp.stack([cos_first, -sin_first], axis=1)
+    spread = jnp.einsum("cab,azk->czkb", rows, first, precision=highest)
+    twisted = jnp.stack(
+        [
+            spread[:, 0] * cos_twist + spread[:, 1] * sin_twist,
+            spread[:, 1] * cos_twist - spread[:, 0] * sin_twist,
+        ],
+        axis=1,
+    )
+    forward = jnp.stack(
+        [jnp.stack([cos_last, -sin_last], axis=1), jnp.stack([sin_last, cos_last], axis=1)], axis=0
+    )
+    spectra = jnp.einsum("czkb,zbwj->cwkj", twisted, forward, precision=highest)
+    sig, ker = spectra[:lanes], spectra[lanes:]
+    product = jnp.stack(
+        [
+            sig[:, 0] * ker[:, 0] - sig[:, 1] * ker[:, 1],
+            sig[:, 0] * ker[:, 1] + sig[:, 1] * ker[:, 0],
+        ],
+        axis=1,
+    )
+    backward = jnp.stack(
+        [jnp.stack([cos_last, sin_last], axis=1), jnp.stack([-sin_last, cos_last], axis=1)], axis=0
+    )
+    partial = jnp.einsum("czkj,zjwm->cwkm", product, backward, precision=highest)
+    untwisted = jnp.stack(
+        [
+            partial[:, 0] * cos_twist - partial[:, 1] * sin_twist,
+            partial[:, 1] * cos_twist + partial[:, 0] * sin_twist,
+        ],
+        axis=1,
+    )
+    last = jnp.stack([cos_first, -sin_first], axis=0)
+    out = jnp.einsum("czkm,zlk->clm", untwisted, last, precision=highest)
     return out.reshape(lanes, length) / points
 
 

time: 365 us -> 369 us (1.011)
  waiting for transfers between devices: 113 us -> 105 us
  other arithmetic: 11.7 us -> 18.9 us
  local copies, waits for them, and re-layouts: 18.4 us -> 24.9 us
    all_to_all x1, waiting for transfers between devices: 8.63 us -> 1.34 us  [causal_convolve(): whole = lax.all_to_all(both, 'ctx', split_axis=1, concat_axis=2, tiled=True)]
    dot_general x12 -> x4, matrix products: 12.6 us -> 9.42 us  [the longest x1 3.17 us: local_convolve(): spectra = jnp.einsum('czkb,zbwj->cwkj', twisted, forward, precision=highest)]
  transfers between devices with their start and end apart: 3 -> 3, of which waited for: 3 -> 3; matrix products, arithmetic and copies ran while one was open for 1% -> 3% of each run, Pallas kernels for 0% -> 0%
where the time goes in v3:
time: 369 us; the launch traced here: 367 us
  blocking collectives  172 us (47%)
  waiting for transfers between devices  105 us (28%)
  local copies, waits for them, and re-layouts  24.9 us (7%)
  starting transfers between devices  23.8 us (6%)
  matrix products  22.4 us (6%)
  other arithmetic  18.9 us (5%)
    all_to_all x1, blocking collectives, token_move(): lax.all_to_all(blocks, ('ctx', 'exp'), split_axis=0, concat_axis=0, tiled...  104 us
    all_to_all x1, waiting for transfers between devices, token_move(): lax.all_to_all(blocks, ('ctx', 'exp'), split_axis=0, concat_axis=0, tiled...  94.8 us
    all_to_all x1, blocking collectives, a2a_reduce(): pieces = lax.all_to_all(sent, axes, 0, 0, tiled=True)  27.7 us
    all_to_all x1, blocking collectives, a2a_allreduce(): gathered = lax.all_to_all(spread, axes, 0, 0, tiled=True)  26.3 us
    all_to_all x1, blocking collectives, causal_convolve(): lax.all_to_all(convolved, 'ctx', split_axis=1, concat_axis=0, tiled=True)  13.5 us
    all_to_all x1, starting transfers between devices, causal_convolve(): whole = lax.all_to_all(both, 'ctx', split_axis=1, concat_axis=2, tiled=True)  10.2 us
    all_to_all x1, waiting for transfers between devices, a2a_reduce(): pieces = lax.all_to_all(sent, axes, 0, 0, tiled=True)  8.75 us
  transfers between devices with their start and end apart: 3, of which 3 were waited for; matrix products, arithmetic and copies ran while one was open for 3% of the time, Pallas kernels for 0%

profile of v3, /device:TPU:1, one launch (start us, length us, event | category | flops | bytes accessed | tf_op | source)
XLA Modules:
  0.0 367.4 jit_solution(3291590175762926204)
XLA Ops:
  2.8 1.7 fusion.39
  5.3 1.8 copy.47
  7.1 10.2 %all-to-all-start = ((f32[2,256,128]{2,0,1:T(2,128)}), f32[2,256,128]{2,0,1:T(2,128)}, u32[]{:S(2)}, u32[]{:S(2)}) async-start(f32[2,256,128]{2,0,1:T(2,128)} %copy.47), calls=%async_computation | async-start | bytes 524288 | tf_op jit(solution)/shard_map/all_to_all | solution.py:113
  28.4 1.7 concatenate.9
  31.7 1.7 concatenate.8
  33.4 2.9 convolution_bitcast_fusion
  37.6 3.2 fusion.8
  42.4 2.3 fusion.18
  44.6 1.7 div.112
  47.3 13.5 %all_to_all.56 = f32[16,16,128]{2,0,1:T(8,128)} all-to-all(f32[16,16,128]{2,0,1:T(8,128)S(1)} %copy.57), channel_id=1, replica_groups=mesh['ctx'=16,'exp'=8,'rep'=2] {'ctx'}, dimensions={1} | all-to-all | bytes 262144 | tf_op jit(solution)/shard_map/all_to_all | solution.py:115
  60.8 1.7 copy.58
  62.4 2.4 convolution_convert_fusion
  64.9 7.0 %all-to-all-start.2 = ((bf16[8,16,2048]{2,1,0:T(8,128)(2,1)}), bf16[8,16,2048]{2,1,0:T(8,128)(2,1)}, u32[]{:S(2)}, u32[]{:S(2)}) async-start(bf16[8,16,2048]{2,1,0:T(8,128)(2,1)} %bitcast.187), calls=%async_computation.2 | async-start | bytes 1048576 | tf_op jit(solution)/shard_map/all_to_all | solution.py:37
  72.6 8.7 %all-to-all-done.2 = bf16[8,16,2048]{2,1,0:T(8,128)(2,1)} async-done(((bf16[8,16,2048]{2,1,0:T(8,128)(2,1)}), bf16[8,16,2048]{2,1,0:T(8,128)(2,1)}, u32[]{:S(2)}, u32[]{:S(2)}) %all-to-all-start.2) | async-done | bytes 524320 | tf_op jit(solution)/shard_map/all_to_all | solution.py:37
  84.3 104.0 %all_to_all.57 = bf16[128,8,2048]{2,1,0:T(8,128)(2,1)S(1)} all-to-all(bf16[128,8,2048]{2,1,0:T(8,128)(2,1)S(1)} %bitcast.184), channel_id=1, replica_groups=mesh['ctx'=16,'exp'=8,'rep'=2] {'ctx','exp'}, dimensions={0} | all-to-all | bytes 8388608 | tf_op jit(solution)/shard_map/all_to_all | solution.py:54
  190.9 3.2 convert_bitcast_fusion
  194.1 6.6 %all-to-all-start.4 = ((bf16[128,8,2048]{2,1,0:T(8,128)(2,1)}), bf16[128,8,2048]{2,1,0:T(8,128)(2,1)}, u32[]{:S(2)}, u32[]{:S(2)}) async-start(bf16[128,8,2048]{2,1,0:T(8,128)(2,1)} %convert_bitcast_fusion), calls=%async_computation.4 | async-start | bytes 8388608 | tf_op jit(solution)/shard_map/all_to_all | solution.py:54
  203.2 94.8 %all-to-all-done.4 = bf16[128,8,2048]{2,1,0:T(8,128)(2,1)} async-done(((bf16[128,8,2048]{2,1,0:T(8,128)(2,1)}), bf16[128,8,2048]{2,1,0:T(8,128)(2,1)}, u32[]{:S(2)}, u32[]{:S(2)}) %all-to-all-start.4) | async-done | bytes 4194336 | tf_op jit(solution)/shard_map/all_to_all | solution.py:54
  298.0 3.0 reduce_sum.64
  303.8 2.6 convolution_convert_fusion.1
  306.4 2.0 copy.61
  308.4 27.7 %all_to_all.58 = bf16[256,8,112]{2,1,0:T(8,128)(2,1)} all-to-all(bf16[256,8,112]{2,1,0:T(8,128)(2,1)} %bitcast.188), channel_id=1, replica_groups=mesh['ctx'=16,'exp'=8,'rep'=2] {'ctx','exp','rep'}, dimensions={0} | all-to-all | bytes 917504 | tf_op jit(solution)/shard_map/all_to_all | solution.py:37
  337.6 26.3 %all_to_all.59 = bf16[256,8,112]{2,1,0:T(8,128)(2,1)S(1)} all-to-all(bf16[256,8,112]{2,1,0:T(8,128)(2,1)S(1)} %broadcast_in_dim.21), channel_id=1, replica_groups=mesh['ctx'=16,'exp'=8,'rep'=2] {'ctx','exp','rep'}, dimensions={0} | all-to-all | bytes 917504 | tf_op jit(solution)/shard_map/all_to_all | solution.py:49
  364.9 2.5 copy.62
  (87 shorter events, 33.2 us)
Async XLA Ops:
  0.6 2.2 copy-start
  2.0 2.4 copy-start.9
  7.1 19.0 %all-to-all-start = ((f32[2,256,128]{2,0,1:T(2,128)}), f32[2,256,128]{2,0,1:T(2,128)}, u32[]{:S(2)}, u32[]{:S(2)}) async-start(f32[2,256,128]{2,0,1:T(2,128)} %copy.47), calls=%async_computation | async-start | bytes 524288 | tf_op jit(solution)/shard_map/all_to_all | solution.py:113
  33.4 4.2 %copy-start.3 = (f32[1,64,2,64]{1,3,0,2:T(8,128)S(1)}, f32[1,64,2,64]{1,3,0,2:T(8,128)}, u32[]{:S(2)}) copy-start(f32[1,64,2,64]{1,3,0,2:T(8,128)} %get-tuple-element.22) | copy-start | bytes 98308
  33.4 4.2 %copy-start.4 = (f32[1,64,2,64]{1,3,0,2:T(8,128)S(1)}, f32[1,64,2,64]{1,3,0,2:T(8,128)}, u32[]{:S(2)}) copy-start(f32[1,64,2,64]{1,3,0,2:T(8,128)} %get-tuple-element.25) | copy-start | bytes 98308
  37.6 3.5 copy-start.5
  37.6 3.5 copy-start.6
  40.8 1.4 copy-start.7
  40.8 1.4 copy-start.8
  40.8 1.5 copy-start.10
  44.6 38.8 %copy-start.13 = (f32[2048]{0:T(1024)S(1)}, f32[2048]{0:T(1024)}, u32[]{:S(2)}) copy-start(f32[2048]{0:T(1024)} %param.25) | copy-start | bytes 24580
  64.9 16.4 %all-to-all-start.2 = ((bf16[8,16,2048]{2,1,0:T(8,128)(2,1)}), bf16[8,16,2048]{2,1,0:T(8,128)(2,1)}, u32[]{:S(2)}, u32[]{:S(2)}) async-start(bf16[8,16,2048]{2,1,0:T(8,128)(2,1)} %bitcast.187), calls=%async_computation.2 | async-start | bytes 1048576 | tf_op jit(solution)/shard_map/all_to_all | solution.py:37
  84.2 104.0 %copy-start.14 = (bf16[1,2048,256]{2,1,0:T(8,128)(2,1)S(1)}, bf16[1,2048,256]{2,1,0:T(8,128)(2,1)}, u32[]{:S(2)}) copy-start(bf16[1,2048,256]{2,1,0:T(8,128)(2,1)} %param.27) | copy-start | bytes 3145732
  188.3 1.3 copy-start.15
  189.6 1.3 copy-start.1
  194.1 6.7 %copy-start.11 = (s32[1,16,2]{1,2,0:T(2,128)S(1)}, s32[1,16,2]{1,2,0:T(2,128)}, u32[]{:S(2)}) copy-start(s32[1,16,2]{1,2,0:T(2,128)} %param.30) | copy-start | bytes 388
  194.1 7.4 %copy-start.16 = (bf16[2048,8]{0,1:T(8,128)(2,1)S(1)}, bf16[2048,8]{0,1:T(8,128)(2,1)}, u32[]{:S(2)}) copy-start(bf16[2048,8]{0,1:T(8,128)(2,1)} %param.26) | copy-start | bytes 98308
  194.1 103.9 %all-to-all-start.4 = ((bf16[128,8,2048]{2,1,0:T(8,128)(2,1)}), bf16[128,8,2048]{2,1,0:T(8,128)(2,1)}, u32[]{:S(2)}, u32[]{:S(2)}) async-start(bf16[128,8,2048]{2,1,0:T(8,128)(2,1)} %convert_bitcast_fusion), calls=%async_computation.4 | async-start | bytes 8388608 | tf_op jit(solution)/shard_map/all_to_all | solution.py:54
  202.4 101.4 %copy-start.12 = (f32[1,16,112]{2,1,0:T(8,128)S(1)}, f32[1,16,112]{2,1,0:T(8,128)}, u32[]{:S(2)}) copy-start(f32[1,16,112]{2,1,0:T(8,128)} %param.33) | copy-start | bytes 21508
  303.8 61.1 %copy-start.2 = (bf16[16,2048]{1,0:T(8,128)(2,1)}, bf16[16,2048]{1,0:T(8,128)(2,1)S(1)}, u32[]{:S(2)}) copy-start(bf16[16,2048]{1,0:T(8,128)(2,1)S(1)} %fusion.49) | copy-start | bytes 196612

commit v4 on v2

--- a/solution.py
+++ b/solution.py
@@ -54,16 +54,16 @@
     return lax.all_to_all(blocks, ("ctx", "exp"), split_axis=0, concat_axis=0, tiled=True)
 
 
-def local_convolve(signal, kernel):
+def local_convolve(whole):
     highest = lax.Precision.HIGHEST
-    lanes, length = signal.shape
+    _, lanes, length = whole.shape
     points = 2 * length
     outer = int(round(math.sqrt(points)))
     while points % outer:
         outer -= 1
     inner = points // outer
     half = length // inner
-    rows = jnp.concatenate([signal, kernel], axis=0).reshape(2 * lanes, half, inner)
+    rows = whole.reshape(2 * lanes, half, inner)
     a_ids = jnp.arange(half, dtype=jnp.int32)
     k1_ids = jnp.arange(outer, dtype=jnp.int32)
     b_ids = jnp.arange(inner, dtype=jnp.int32)
@@ -100,7 +100,7 @@
 def causal_convolve(source, shaped):
     both = jnp.stack([source.T, shaped.T], axis=0)
     whole = lax.all_to_all(both, "ctx", split_axis=1, concat_axis=2, tiled=True)
-    convolved = local_convolve(whole[0], whole[1])
+    convolved = local_convolve(whole)
     back = lax.all_to_all(convolved, "ctx", split_axis=1, concat_axis=0, tiled=True)
     return back.T
 

time: 365 us -> 360 us (0.986)
  local copies, waits for them, and re-layouts: 18.4 us -> 13 us
where the time goes in v4:
time: 360 us; the launch traced here: 359 us
  blocking collectives  171 us (48%)
  waiting for transfers between devices  113 us (31%)
  matrix products  25.7 us (7%)
  starting transfers between devices  23.6 us (7%)
  local copies, waits for them, and re-layouts  13 us (4%)
  other arithmetic  11.6 us (3%)
    all_to_all x1, blocking collectives, token_move(): lax.all_to_all(blocks, ('ctx', 'exp'), split_axis=0, concat_axis=0, tiled...  104 us
    all_to_all x1, waiting for transfers between devices, token_move(): lax.all_to_all(blocks, ('ctx', 'exp'), split_axis=0, concat_axis=0, tiled...  94.8 us
    all_to_all x1, blocking collectives, a2a_reduce(): pieces = lax.all_to_all(sent, axes, 0, 0, tiled=True)  27.8 us
    all_to_all x1, blocking collectives, a2a_allreduce(): gathered = lax.all_to_all(spread, axes, 0, 0, tiled=True)  26.3 us
    all_to_all x1, blocking collectives, causal_convolve(): lax.all_to_all(convolved, 'ctx', split_axis=1, concat_axis=0, tiled=True)  12.6 us
    all_to_all x1, starting transfers between devices, causal_convolve(): whole = lax.all_to_all(both, 'ctx', split_axis=1, concat_axis=2, tiled=True)  10.1 us
    all_to_all x1, waiting for transfers between devices, a2a_reduce(): pieces = lax.all_to_all(sent, axes, 0, 0, tiled=True)  9.42 us
    all_to_all x1, waiting for transfers between devices, causal_convolve(): whole = lax.all_to_all(both, 'ctx', split_axis=1, concat_axis=2, tiled=True)  8.63 us
  transfers between devices with their start and end apart: 3, of which 3 were waited for; matrix products, arithmetic and copies ran while one was open for 1% of the time, Pallas kernels for 0%

profile of v4, /device:TPU:1, one launch (start us, length us, event | category | flops | bytes accessed | tf_op | source)
XLA Modules:
  0.0 358.5 jit_solution(790152852751016245)
XLA Ops:
  0.7 1.4 fusion.22
  2.7 1.7 fusion.35
  6.2 10.1 %all-to-all-start = ((f32[2,256,128]{2,0,1:T(2,128)}), f32[2,256,128]{2,0,1:T(2,128)S(1)}, u32[]{:S(2)}, u32[]{:S(2)}) async-start(f32[2,256,128]{2,0,1:T(2,128)} %copy.30), calls=%async_computation | async-start | bytes 524288 | tf_op jit(solution)/shard_map/all_to_all | solution.py:102
  16.4 8.6 %all-to-all-done = f32[2,256,128]{2,0,1:T(2,128)S(1)} async-done(((f32[2,256,128]{2,0,1:T(2,128)}), f32[2,256,128]{2,0,1:T(2,128)S(1)}, u32[]{:S(2)}, u32[]{:S(2)}) %all-to-all-start) | async-done | bytes 262176 | tf_op jit(solution)/shard_map/all_to_all | solution.py:102
  26.1 2.1 fusion.90
  28.3 2.1 convolution_negate_fusion
  40.8 12.6 %all_to_all.56 = f32[16,16,128]{2,0,1:T(8,128)S(1)} all-to-all(f32[16,16,128]{2,0,1:T(8,128)S(1)} %copy.33), channel_id=1, replica_groups=mesh['ctx'=16,'exp'=8,'rep'=2] {'ctx'}, dimensions={1} | all-to-all | bytes 262144 | tf_op jit(solution)/shard_map/all_to_all | solution.py:104
  53.6 2.5 convolution_convert_fusion
  56.1 6.8 %all-to-all-start.2 = ((bf16[8,16,2048]{2,1,0:T(8,128)(2,1)}), bf16[8,16,2048]{2,1,0:T(8,128)(2,1)}, u32[]{:S(2)}, u32[]{:S(2)}) async-start(bf16[8,16,2048]{2,1,0:T(8,128)(2,1)} %bitcast.167), calls=%async_computation.2 | async-start | bytes 1048576 | tf_op jit(solution)/shard_map/all_to_all | solution.py:37
  63.0 9.4 %all-to-all-done.2 = bf16[8,16,2048]{2,1,0:T(8,128)(2,1)} async-done(((bf16[8,16,2048]{2,1,0:T(8,128)(2,1)}), bf16[8,16,2048]{2,1,0:T(8,128)(2,1)}, u32[]{:S(2)}, u32[]{:S(2)}) %all-to-all-start.2) | async-done | bytes 524320 | tf_op jit(solution)/shard_map/all_to_all | solution.py:37
  75.4 104.0 %all_to_all.57 = bf16[128,8,2048]{2,1,0:T(8,128)(2,1)S(1)} all-to-all(bf16[128,8,2048]{2,1,0:T(8,128)(2,1)S(1)} %bitcast.164), channel_id=1, replica_groups=mesh['ctx'=16,'exp'=8,'rep'=2] {'ctx','exp'}, dimensions={0} | all-to-all | bytes 8388608 | tf_op jit(solution)/shard_map/all_to_all | solution.py:54
  179.4 1.3 fusion.2
  180.7 1.3 fusion.8
  182.0 3.2 convert_bitcast_fusion
  185.2 6.7 %all-to-all-start.4 = ((bf16[128,8,2048]{2,1,0:T(8,128)(2,1)}), bf16[128,8,2048]{2,1,0:T(8,128)(2,1)}, u32[]{:S(2)}, u32[]{:S(2)}) async-start(bf16[128,8,2048]{2,1,0:T(8,128)(2,1)} %convert_bitcast_fusion), calls=%async_computation.4 | async-start | bytes 8388608 | tf_op jit(solution)/shard_map/all_to_all | solution.py:54
  194.3 94.8 %all-to-all-done.4 = bf16[128,8,2048]{2,1,0:T(8,128)(2,1)} async-done(((bf16[128,8,2048]{2,1,0:T(8,128)(2,1)}), bf16[128,8,2048]{2,1,0:T(8,128)(2,1)}, u32[]{:S(2)}, u32[]{:S(2)}) %all-to-all-start.4) | async-done | bytes 4194336 | tf_op jit(solution)/shard_map/all_to_all | solution.py:54
  289.1 3.0 reduce_sum.64
  292.7 1.2 gather_fusion.1
  294.9 2.6 convolution_convert_fusion.1
  297.5 2.0 copy.37
  299.6 27.8 %all_to_all.58 = bf16[256,8,112]{2,1,0:T(8,128)(2,1)} all-to-all(bf16[256,8,112]{2,1,0:T(8,128)(2,1)} %bitcast.168), channel_id=1, replica_groups=mesh['ctx'=16,'exp'=8,'rep'=2] {'ctx','exp','rep'}, dimensions={0} | all-to-all | bytes 917504 | tf_op jit(solution)/shard_map/all_to_all | solution.py:37
  327.3 1.3 reduce_sum.65
  328.7 26.3 %all_to_all.59 = bf16[256,8,112]{2,1,0:T(8,128)(2,1)S(1)} all-to-all(bf16[256,8,112]{2,1,0:T(8,128)(2,1)S(1)} %broadcast_in_dim.21), channel_id=1, replica_groups=mesh['ctx'=16,'exp'=8,'rep'=2] {'ctx','exp','rep'}, dimensions={0} | all-to-all | bytes 917504 | tf_op jit(solution)/shard_map/all_to_all | solution.py:49
  356.0 2.5 copy.38
  (75 shorter events, 22.0 us)
Async XLA Ops:
  0.6 2.1 copy-start
  0.6 4.5 %copy-start.4 = (f32[128,256]{1,0:T(8,128)S(1)}, f32[128,256]{1,0:T(8,128)}, u32[]{:S(2)}) copy-start(f32[128,256]{1,0:T(8,128)} %param.21) | copy-start | bytes 393220
  4.4 0.7 copy-start.1
  6.2 18.9 %all-to-all-start = ((f32[2,256,128]{2,0,1:T(2,128)}), f32[2,256,128]{2,0,1:T(2,128)S(1)}, u32[]{:S(2)}, u32[]{:S(2)}) async-start(f32[2,256,128]{2,0,1:T(2,128)} %copy.30), calls=%async_computation | async-start | bytes 524288 | tf_op jit(solution)/shard_map/all_to_all | solution.py:102
  35.9 17.6 %copy-start.8 = (f32[256]{0:T(256)S(1)}, f32[256]{0:T(256)}, u32[]{:S(2)}) copy-start(f32[256]{0:T(256)} %param.23) | copy-start | bytes 3076
  37.3 25.6 %copy-start.5 = (s32[1,16,2]{1,2,0:T(2,128)S(1)}, s32[1,16,2]{1,2,0:T(2,128)}, u32[]{:S(2)}) copy-start(s32[1,16,2]{1,2,0:T(2,128)} %param.30) | copy-start | bytes 388
  37.4 25.6 %copy-start.9 = (s32[1,16,2]{1,2,0:T(2,128)S(1)}, s32[1,16,2]{1,2,0:T(2,128)}, u32[]{:S(2)}) copy-start(s32[1,16,2]{1,2,0:T(2,128)} %param.31) | copy-start | bytes 388
  38.1 36.5 %copy-start.7 = (f32[2048]{0:T(1024)S(1)}, f32[2048]{0:T(1024)}, u32[]{:S(2)}) copy-start(f32[2048]{0:T(1024)} %param.25) | copy-start | bytes 24580
  56.1 16.3 %all-to-all-start.2 = ((bf16[8,16,2048]{2,1,0:T(8,128)(2,1)}), bf16[8,16,2048]{2,1,0:T(8,128)(2,1)}, u32[]{:S(2)}, u32[]{:S(2)}) async-start(bf16[8,16,2048]{2,1,0:T(8,128)(2,1)} %bitcast.167), calls=%async_computation.2 | async-start | bytes 1048576 | tf_op jit(solution)/shard_map/all_to_all | solution.py:37
  75.3 104.0 %copy-start.10 = (bf16[1,2048,256]{2,1,0:T(8,128)(2,1)S(1)}, bf16[1,2048,256]{2,1,0:T(8,128)(2,1)}, u32[]{:S(2)}) copy-start(bf16[1,2048,256]{2,1,0:T(8,128)(2,1)} %param.27) | copy-start | bytes 3145732
  179.4 1.3 copy-start.11
  180.7 1.3 copy-start.2
  185.2 7.4 %copy-start.12 = (bf16[2048,8]{0,1:T(8,128)(2,1)S(1)}, bf16[2048,8]{0,1:T(8,128)(2,1)}, u32[]{:S(2)}) copy-start(bf16[2048,8]{0,1:T(8,128)(2,1)} %param.26) | copy-start | bytes 98308
  185.2 103.9 %all-to-all-start.4 = ((bf16[128,8,2048]{2,1,0:T(8,128)(2,1)}), bf16[128,8,2048]{2,1,0:T(8,128)(2,1)}, u32[]{:S(2)}, u32[]{:S(2)}) async-start(bf16[128,8,2048]{2,1,0:T(8,128)(2,1)} %convert_bitcast_fusion), calls=%async_computation.4 | async-start | bytes 8388608 | tf_op jit(solution)/shard_map/all_to_all | solution.py:54
  193.5 101.4 %copy-start.6 = (f32[1,16,112]{2,1,0:T(8,128)S(1)}, f32[1,16,112]{2,1,0:T(8,128)}, u32[]{:S(2)}) copy-start(f32[1,16,112]{2,1,0:T(8,128)} %param.33) | copy-start | bytes 21508
  294.9 63.6 %copy-start.3 = (bf16[16,2048]{1,0:T(8,128)(2,1)}, bf16[16,2048]{1,0:T(8,128)(2,1)S(1)}, u32[]{:S(2)}) copy-start(bf16[16,2048]{1,0:T(8,128)(2,1)S(1)} %fusion.54) | copy-start | bytes 196612

commit v5 on v4

--- a/solution.py
+++ b/solution.py
@@ -98,11 +98,10 @@
 
 
 def causal_convolve(source, shaped):
-    both = jnp.stack([source.T, shaped.T], axis=0)
+    both = jnp.stack([source, shaped], axis=0)
     whole = lax.all_to_all(both, "ctx", split_axis=1, concat_axis=2, tiled=True)
     convolved = local_convolve(whole)
-    back = lax.all_to_all(convolved, "ctx", split_axis=1, concat_axis=0, tiled=True)
-    return back.T
+    return lax.all_to_all(convolved, "ctx", split_axis=1, concat_axis=0, tiled=True)
 
 
 def shards(
@@ -132,13 +131,13 @@
     own_rows = local_rows // exp_count
     length = local_rows * ctx_count
     normed = rms_scale(local_x, norm1_gain)
-    projected = jnp.einsum("ti,igd->tgd", normed, w_in, preferred_element_type=jnp.float32)
-    source = projected[:, 1] * projected[:, 0]
+    projected = jnp.einsum("ti,igd->gdt", normed, w_in, preferred_element_type=jnp.float32)
+    source = projected[1] * projected[0]
     positions = (ctx_pos * local_rows + jnp.arange(local_rows, dtype=jnp.int32)).astype(jnp.float32)
-    shaped = long_filter * jnp.exp(-filter_decay[None, :] * positions[:, None] / length)
+    shaped = long_filter.T * jnp.exp(-filter_decay[:, None] * positions[None, :] / length)
     convolved = causal_convolve(source, shaped)
-    gated_rows = (projected[:, 2] * (convolved + conv_bias[None, :] * source)).astype(jnp.bfloat16)
-    mixed_full = jnp.dot(gated_rows, w_out, preferred_element_type=jnp.float32)
+    gated_rows = (projected[2] * (convolved + conv_bias[:, None] * source)).astype(jnp.bfloat16)
+    mixed_full = jnp.einsum("dt,de->te", gated_rows, w_out, preferred_element_type=jnp.float32)
     mixed_sum = a2a_reduce(mixed_full, "exp", jnp.bfloat16)
     residual_rows = lax.dynamic_slice_in_dim(local_x, exp_pos * own_rows, own_rows, 0)
     hidden_state = stored(residual_rows.astype(jnp.float32) + mixed_sum)

time: 360 us -> 368 us (1.022)
  local copies, waits for them, and re-layouts: 13 us -> 18.5 us
where the time goes in v5:
time: 368 us; the launch traced here: 367 us
  blocking collectives  171 us (46%)
  waiting for transfers between devices  111 us (30%)
  matrix products  26.9 us (7%)
  starting transfers between devices  23.6 us (6%)
  local copies, waits for them, and re-layouts  18.5 us (5%)
  other arithmetic  15.2 us (4%)
    all_to_all x1, blocking collectives, token_move(): lax.all_to_all(blocks, ('ctx', 'exp'), split_axis=0, concat_axis=0, tiled...  104 us
    all_to_all x1, waiting for transfers between devices, token_move(): lax.all_to_all(blocks, ('ctx', 'exp'), split_axis=0, concat_axis=0, tiled...  94.2 us
    all_to_all x1, blocking collectives, a2a_reduce(): pieces = lax.all_to_all(sent, axes, 0, 0, tiled=True)  27.8 us
    all_to_all x1, blocking collectives, a2a_allreduce(): gathered = lax.all_to_all(spread, axes, 0, 0, tiled=True)  26.3 us
    all_to_all x1, blocking collectives, causal_convolve(): lax.all_to_all(convolved, 'ctx', split_axis=1, concat_axis=0, tiled=True)  12.8 us
    all_to_all x1, starting transfers between devices, causal_convolve(): whole = lax.all_to_all(both, 'ctx', split_axis=1, concat_axis=2, tiled=True)  10.2 us
    all_to_all x1, waiting for transfers between devices, a2a_reduce(): pieces = lax.all_to_all(sent, axes, 0, 0, tiled=True)  8.76 us
    all_to_all x1, waiting for transfers between devices, causal_convolve(): whole = lax.all_to_all(both, 'ctx', split_axis=1, concat_axis=2, tiled=True)  8.07 us
  transfers between devices with their start and end apart: 3, of which 3 were waited for; matrix products, arithmetic and copies ran while one was open for 1% of the time, Pallas kernels for 0%

profile of v5, /device:TPU:1, one launch (start us, length us, event | category | flops | bytes accessed | tf_op | source)
XLA Modules:
  0.0 367.1 jit_solution(13837486091757355787)
XLA Ops:
  2.8 1.7 convolution_bitcast_fusion
  5.3 1.8 copy.30
  7.1 10.2 %all-to-all-start = ((f32[2,256,128]{2,0,1:T(2,128)}), f32[2,256,128]{2,0,1:T(2,128)}, u32[]{:S(2)}, u32[]{:S(2)}) async-start(f32[2,256,128]{2,0,1:T(2,128)} %copy.30), calls=%async_computation | async-start | bytes 524288 | tf_op jit(solution)/shard_map/all_to_all | solution.py:102
  18.1 8.1 %all-to-all-done = f32[2,256,128]{2,0,1:T(2,128)} async-done(((f32[2,256,128]{2,0,1:T(2,128)}), f32[2,256,128]{2,0,1:T(2,128)}, u32[]{:S(2)}, u32[]{:S(2)}) %all-to-all-start) | async-done | bytes 262176 | tf_op jit(solution)/shard_map/all_to_all | solution.py:102
  27.9 1.9 reshape.152
  29.8 2.1 fusion.89
  31.9 2.1 convolution_negate_fusion
  34.1 1.9 fusion.29
  44.3 1.7 div.108
  46.9 12.8 %all_to_all.56 = f32[16,16,128]{2,0,1:T(8,128)} all-to-all(f32[16,16,128]{2,0,1:T(8,128)S(1)} %copy.33), channel_id=1, replica_groups=mesh['ctx'=16,'exp'=8,'rep'=2] {'ctx'}, dimensions={1} | all-to-all | bytes 262144 | tf_op jit(solution)/shard_map/all_to_all | solution.py:104
  59.7 1.7 copy.34
  62.3 2.3 convolution_convert_fusion
  64.6 6.8 %all-to-all-start.2 = ((bf16[8,16,2048]{2,1,0:T(8,128)(2,1)}), bf16[8,16,2048]{2,1,0:T(8,128)(2,1)}, u32[]{:S(2)}, u32[]{:S(2)}) async-start(bf16[8,16,2048]{2,1,0:T(8,128)(2,1)} %convolution_convert_fusion), calls=%async_computation.2 | async-start | bytes 1048576 | tf_op jit(solution)/shard_map/all_to_all | solution.py:37
  72.1 8.8 %all-to-all-done.2 = bf16[8,16,2048]{2,1,0:T(8,128)(2,1)} async-done(((bf16[8,16,2048]{2,1,0:T(8,128)(2,1)}), bf16[8,16,2048]{2,1,0:T(8,128)(2,1)}, u32[]{:S(2)}, u32[]{:S(2)}) %all-to-all-start.2) | async-done | bytes 524320 | tf_op jit(solution)/shard_map/all_to_all | solution.py:37
  83.8 104.0 %all_to_all.57 = bf16[128,8,2048]{2,1,0:T(8,128)(2,1)S(1)} all-to-all(bf16[128,8,2048]{2,1,0:T(8,128)(2,1)S(1)} %bitcast.163), channel_id=1, replica_groups=mesh['ctx'=16,'exp'=8,'rep'=2] {'ctx','exp'}, dimensions={0} | all-to-all | bytes 8388608 | tf_op jit(solution)/shard_map/all_to_all | solution.py:54
  190.4 3.2 convert_bitcast_fusion
  193.7 6.7 %all-to-all-start.4 = ((bf16[128,8,2048]{2,1,0:T(8,128)(2,1)}), bf16[128,8,2048]{2,1,0:T(8,128)(2,1)}, u32[]{:S(2)}, u32[]{:S(2)}) async-start(bf16[128,8,2048]{2,1,0:T(8,128)(2,1)} %convert_bitcast_fusion), calls=%async_computation.4 | async-start | bytes 8388608 | tf_op jit(solution)/shard_map/all_to_all | solution.py:54
  203.4 94.2 %all-to-all-done.4 = bf16[128,8,2048]{2,1,0:T(8,128)(2,1)} async-done(((bf16[128,8,2048]{2,1,0:T(8,128)(2,1)}), bf16[128,8,2048]{2,1,0:T(8,128)(2,1)}, u32[]{:S(2)}, u32[]{:S(2)}) %all-to-all-start.4) | async-done | bytes 4194336 | tf_op jit(solution)/shard_map/all_to_all | solution.py:54
  297.6 3.0 reduce_sum.64
  303.5 2.6 convolution_convert_fusion.1
  306.1 2.0 copy.37
  308.1 27.8 %all_to_all.58 = bf16[256,8,112]{2,1,0:T(8,128)(2,1)} all-to-all(bf16[256,8,112]{2,1,0:T(8,128)(2,1)} %bitcast.166), channel_id=1, replica_groups=mesh['ctx'=16,'exp'=8,'rep'=2] {'ctx','exp','rep'}, dimensions={0} | all-to-all | bytes 917504 | tf_op jit(solution)/shard_map/all_to_all | solution.py:37
  337.3 26.3 %all_to_all.59 = bf16[256,8,112]{2,1,0:T(8,128)(2,1)S(1)} all-to-all(bf16[256,8,112]{2,1,0:T(8,128)(2,1)S(1)} %broadcast_in_dim.21), channel_id=1, replica_groups=mesh['ctx'=16,'exp'=8,'rep'=2] {'ctx','exp','rep'}, dimensions={0} | all-to-all | bytes 917504 | tf_op jit(solution)/shard_map/all_to_all | solution.py:49
  364.6 2.5 copy.38
  (76 shorter events, 30.0 us)
Async XLA Ops:
  0.6 2.2 copy-start
  2.0 2.4 copy-start.5
  7.1 19.0 %all-to-all-start = ((f32[2,256,128]{2,0,1:T(2,128)}), f32[2,256,128]{2,0,1:T(2,128)}, u32[]{:S(2)}, u32[]{:S(2)}) async-start(f32[2,256,128]{2,0,1:T(2,128)} %copy.30), calls=%async_computation | async-start | bytes 524288 | tf_op jit(solution)/shard_map/all_to_all | solution.py:102
  29.8 6.2 %copy-start.1 = (f32[64,64]{1,0:T(8,128)S(1)}, f32[64,64]{1,0:T(8,128)}, u32[]{:S(2)}) copy-start(f32[64,64]{1,0:T(8,128)} %get-tuple-element.21) | copy-start | bytes 49156
  29.8 6.2 %copy-start.2 = (f32[64,64]{1,0:T(8,128)S(1)}, f32[64,64]{1,0:T(8,128)}, u32[]{:S(2)}) copy-start(f32[64,64]{1,0:T(8,128)} %get-tuple-element.22) | copy-start | bytes 49156
  40.4 20.9 %copy-start.9 = (f32[256]{0:T(256)S(1)}, f32[256]{0:T(256)}, u32[]{:S(2)}) copy-start(f32[256]{0:T(256)} %param.23) | copy-start | bytes 3076
  41.8 29.6 %copy-start.6 = (s32[1,16,2]{1,2,0:T(2,128)S(1)}, s32[1,16,2]{1,2,0:T(2,128)}, u32[]{:S(2)}) copy-start(s32[1,16,2]{1,2,0:T(2,128)} %param.30) | copy-start | bytes 388
  42.5 40.5 %copy-start.8 = (f32[2048]{0:T(1024)S(1)}, f32[2048]{0:T(1024)}, u32[]{:S(2)}) copy-start(f32[2048]{0:T(1024)} %param.25) | copy-start | bytes 24580
  64.6 16.3 %all-to-all-start.2 = ((bf16[8,16,2048]{2,1,0:T(8,128)(2,1)}), bf16[8,16,2048]{2,1,0:T(8,128)(2,1)}, u32[]{:S(2)}, u32[]{:S(2)}) async-start(bf16[8,16,2048]{2,1,0:T(8,128)(2,1)} %convolution_convert_fusion), calls=%async_computation.2 | async-start | bytes 1048576 | tf_op jit(solution)/shard_map/all_to_all | solution.py:37
  83.8 104.0 %copy-start.10 = (bf16[1,2048,256]{2,1,0:T(8,128)(2,1)S(1)}, bf16[1,2048,256]{2,1,0:T(8,128)(2,1)}, u32[]{:S(2)}) copy-start(bf16[1,2048,256]{2,1,0:T(8,128)(2,1)} %param.27) | copy-start | bytes 3145732
  187.8 1.3 copy-start.11
  189.1 1.3 copy-start.3
  193.7 8.0 %copy-start.12 = (bf16[2048,8]{0,1:T(8,128)(2,1)S(1)}, bf16[2048,8]{0,1:T(8,128)(2,1)}, u32[]{:S(2)}) copy-start(bf16[2048,8]{0,1:T(8,128)(2,1)} %param.26) | copy-start | bytes 98308
  193.7 103.9 %all-to-all-start.4 = ((bf16[128,8,2048]{2,1,0:T(8,128)(2,1)}), bf16[128,8,2048]{2,1,0:T(8,128)(2,1)}, u32[]{:S(2)}, u32[]{:S(2)}) async-start(bf16[128,8,2048]{2,1,0:T(8,128)(2,1)} %convert_bitcast_fusion), calls=%async_computation.4 | async-start | bytes 8388608 | tf_op jit(solution)/shard_map/all_to_all | solution.py:54
  202.6 100.9 %copy-start.7 = (f32[1,16,112]{2,1,0:T(8,128)S(1)}, f32[1,16,112]{2,1,0:T(8,128)}, u32[]{:S(2)}) copy-start(f32[1,16,112]{2,1,0:T(8,128)} %param.33) | copy-start | bytes 21508
  303.5 63.6 %copy-start.4 = (bf16[16,2048]{1,0:T(8,128)(2,1)}, bf16[16,2048]{1,0:T(8,128)(2,1)S(1)}, u32[]{:S(2)}) copy-start(bf16[16,2048]{1,0:T(8,128)(2,1)S(1)} %fusion.54) | copy-start | bytes 196612

commit v6 on v4

--- a/solution.py
+++ b/solution.py
@@ -188,7 +188,7 @@
     loss_scale = 1.0 / math.sqrt(all_tokens)
     usage_grad = ((usage_prob - targets[0]) * loss_scale).astype(jnp.bfloat16)
     local_grad = jnp.einsum(
-        "td,to->do", block_final, usage_grad, preferred_element_type=jnp.float32
+        "td,to->do", block_final, usage_grad, preferred_element_type=jnp.bfloat16
     )
     head_total = a2a_allreduce(local_grad, ("ctx", "exp", "rep"), jnp.bfloat16).T
     return (block_final[None], head_total)

time: 360 us -> 358 us (level)
  no operation moved by 1% of the time
where the time goes in v6:
time: 358 us; the launch traced here: 356 us
  blocking collectives  171 us (48%)
  waiting for transfers between devices  113 us (32%)
  matrix products  25.7 us (7%)
  starting transfers between devices  23.6 us (7%)
  other arithmetic  11.6 us (3%)
  local copies, waits for them, and re-layouts  11 us (3%)
    all_to_all x1, blocking collectives, token_move(): lax.all_to_all(blocks, ('ctx', 'exp'), split_axis=0, concat_axis=0, tiled...  104 us
    all_to_all x1, waiting for transfers between devices, token_move(): lax.all_to_all(blocks, ('ctx', 'exp'), split_axis=0, concat_axis=0, tiled...  94.8 us
    all_to_all x1, blocking collectives, a2a_reduce(): pieces = lax.all_to_all(sent, axes, 0, 0, tiled=True)  27.8 us
    all_to_all x1, blocking collectives, a2a_allreduce(): gathered = lax.all_to_all(spread, axes, 0, 0, tiled=True)  26.3 us
    all_to_all x1, blocking collectives, causal_convolve(): lax.all_to_all(convolved, 'ctx', split_axis=1, concat_axis=0, tiled=True)  12.6 us
    all_to_all x1, starting transfers between devices, causal_convolve(): whole = lax.all_to_all(both, 'ctx', split_axis=1, concat_axis=2, tiled=True)  10.1 us
    all_to_all x1, waiting for transfers between devices, a2a_reduce(): pieces = lax.all_to_all(sent, axes, 0, 0, tiled=True)  9.42 us
    all_to_all x1, waiting for transfers between devices, causal_convolve(): whole = lax.all_to_all(both, 'ctx', split_axis=1, concat_axis=2, tiled=True)  8.63 us
  transfers between devices with their start and end apart: 3, of which 3 were waited for; matrix products, arithmetic and copies ran while one was open for 1% of the time, Pallas kernels for 0%

profile of v6, /device:TPU:1, one launch (start us, length us, event | category | flops | bytes accessed | tf_op | source)
XLA Modules:
  0.0 356.5 jit_solution(12630144481115061823)
XLA Ops:
  0.7 1.4 fusion.22
  2.7 1.7 fusion.35
  6.2 10.1 %all-to-all-start = ((f32[2,256,128]{2,0,1:T(2,128)}), f32[2,256,128]{2,0,1:T(2,128)S(1)}, u32[]{:S(2)}, u32[]{:S(2)}) async-start(f32[2,256,128]{2,0,1:T(2,128)} %copy.30), calls=%async_computation | async-start | bytes 524288 | tf_op jit(solution)/shard_map/all_to_all | solution.py:102
  16.4 8.6 %all-to-all-done = f32[2,256,128]{2,0,1:T(2,128)S(1)} async-done(((f32[2,256,128]{2,0,1:T(2,128)}), f32[2,256,128]{2,0,1:T(2,128)S(1)}, u32[]{:S(2)}, u32[]{:S(2)}) %all-to-all-start) | async-done | bytes 262176 | tf_op jit(solution)/shard_map/all_to_all | solution.py:102
  26.1 2.1 fusion.90
  28.3 2.1 convolution_negate_fusion
  32.7 1.1 convolution_subtract_fusion
  40.8 12.6 %all_to_all.56 = f32[16,16,128]{2,0,1:T(8,128)S(1)} all-to-all(f32[16,16,128]{2,0,1:T(8,128)S(1)} %copy.33), channel_id=1, replica_groups=mesh['ctx'=16,'exp'=8,'rep'=2] {'ctx'}, dimensions={1} | all-to-all | bytes 262144 | tf_op jit(solution)/shard_map/all_to_all | solution.py:104
  53.6 2.5 convolution_convert_fusion
  56.1 6.8 %all-to-all-start.2 = ((bf16[8,16,2048]{2,1,0:T(8,128)(2,1)}), bf16[8,16,2048]{2,1,0:T(8,128)(2,1)}, u32[]{:S(2)}, u32[]{:S(2)}) async-start(bf16[8,16,2048]{2,1,0:T(8,128)(2,1)} %bitcast.168), calls=%async_computation.2 | async-start | bytes 1048576 | tf_op jit(solution)/shard_map/all_to_all | solution.py:37
  63.0 9.4 %all-to-all-done.2 = bf16[8,16,2048]{2,1,0:T(8,128)(2,1)} async-done(((bf16[8,16,2048]{2,1,0:T(8,128)(2,1)}), bf16[8,16,2048]{2,1,0:T(8,128)(2,1)}, u32[]{:S(2)}, u32[]{:S(2)}) %all-to-all-start.2) | async-done | bytes 524320 | tf_op jit(solution)/shard_map/all_to_all | solution.py:37
  75.4 104.0 %all_to_all.57 = bf16[128,8,2048]{2,1,0:T(8,128)(2,1)S(1)} all-to-all(bf16[128,8,2048]{2,1,0:T(8,128)(2,1)S(1)} %bitcast.165), channel_id=1, replica_groups=mesh['ctx'=16,'exp'=8,'rep'=2] {'ctx','exp'}, dimensions={0} | all-to-all | bytes 8388608 | tf_op jit(solution)/shard_map/all_to_all | solution.py:54
  179.4 1.3 fusion.2
  180.7 1.3 fusion.8
  182.0 3.2 convert_bitcast_fusion
  185.2 6.7 %all-to-all-start.4 = ((bf16[128,8,2048]{2,1,0:T(8,128)(2,1)}), bf16[128,8,2048]{2,1,0:T(8,128)(2,1)}, u32[]{:S(2)}, u32[]{:S(2)}) async-start(bf16[128,8,2048]{2,1,0:T(8,128)(2,1)} %convert_bitcast_fusion), calls=%async_computation.4 | async-start | bytes 8388608 | tf_op jit(solution)/shard_map/all_to_all | solution.py:54
  194.3 94.8 %all-to-all-done.4 = bf16[128,8,2048]{2,1,0:T(8,128)(2,1)} async-done(((bf16[128,8,2048]{2,1,0:T(8,128)(2,1)}), bf16[128,8,2048]{2,1,0:T(8,128)(2,1)}, u32[]{:S(2)}, u32[]{:S(2)}) %all-to-all-start.4) | async-done | bytes 4194336 | tf_op jit(solution)/shard_map/all_to_all | solution.py:54
  289.1 3.0 reduce_sum.64
  292.7 1.2 gather_fusion.1
  294.9 2.6 convolution_bitcast_fusion
  297.5 27.8 %all_to_all.58 = bf16[256,8,112]{2,1,0:T(8,128)(2,1)} all-to-all(bf16[256,8,112]{2,1,0:T(8,128)(2,1)} %convolution_bitcast_fusion), channel_id=1, replica_groups=mesh['ctx'=16,'exp'=8,'rep'=2] {'ctx','exp','rep'}, dimensions={0} | all-to-all | bytes 917504 | tf_op jit(solution)/shard_map/all_to_all | solution.py:37
  325.3 1.3 reduce_sum.65
  326.7 26.3 %all_to_all.59 = bf16[256,8,112]{2,1,0:T(8,128)(2,1)S(1)} all-to-all(bf16[256,8,112]{2,1,0:T(8,128)(2,1)S(1)} %broadcast_in_dim.21), channel_id=1, replica_groups=mesh['ctx'=16,'exp'=8,'rep'=2] {'ctx','exp','rep'}, dimensions={0} | all-to-all | bytes 917504 | tf_op jit(solution)/shard_map/all_to_all | solution.py:49
  354.0 2.5 copy.38
  (74 shorter events, 20.9 us)
Async XLA Ops:
  0.6 2.1 copy-start
  0.6 4.5 %copy-start.4 = (f32[128,256]{1,0:T(8,128)S(1)}, f32[128,256]{1,0:T(8,128)}, u32[]{:S(2)}) copy-start(f32[128,256]{1,0:T(8,128)} %param.21) | copy-start | bytes 393220
  4.4 0.7 copy-start.1
  6.2 18.9 %all-to-all-start = ((f32[2,256,128]{2,0,1:T(2,128)}), f32[2,256,128]{2,0,1:T(2,128)S(1)}, u32[]{:S(2)}, u32[]{:S(2)}) async-start(f32[2,256,128]{2,0,1:T(2,128)} %copy.30), calls=%async_computation | async-start | bytes 524288 | tf_op jit(solution)/shard_map/all_to_all | solution.py:102
  35.9 17.6 %copy-start.8 = (f32[256]{0:T(256)S(1)}, f32[256]{0:T(256)}, u32[]{:S(2)}) copy-start(f32[256]{0:T(256)} %param.23) | copy-start | bytes 3076
  37.3 25.6 %copy-start.5 = (s32[1,16,2]{1,2,0:T(2,128)S(1)}, s32[1,16,2]{1,2,0:T(2,128)}, u32[]{:S(2)}) copy-start(s32[1,16,2]{1,2,0:T(2,128)} %param.30) | copy-start | bytes 388
  37.4 25.6 %copy-start.9 = (s32[1,16,2]{1,2,0:T(2,128)S(1)}, s32[1,16,2]{1,2,0:T(2,128)}, u32[]{:S(2)}) copy-start(s32[1,16,2]{1,2,0:T(2,128)} %param.31) | copy-start | bytes 388
  38.1 36.5 %copy-start.7 = (f32[2048]{0:T(1024)S(1)}, f32[2048]{0:T(1024)}, u32[]{:S(2)}) copy-start(f32[2048]{0:T(1024)} %param.25) | copy-start | bytes 24580
  56.1 16.3 %all-to-all-start.2 = ((bf16[8,16,2048]{2,1,0:T(8,128)(2,1)}), bf16[8,16,2048]{2,1,0:T(8,128)(2,1)}, u32[]{:S(2)}, u32[]{:S(2)}) async-start(bf16[8,16,2048]{2,1,0:T(8,128)(2,1)} %bitcast.168), calls=%async_computation.2 | async-start | bytes 1048576 | tf_op jit(solution)/shard_map/all_to_all | solution.py:37
  75.3 104.0 %copy-start.10 = (bf16[1,2048,256]{2,1,0:T(8,128)(2,1)S(1)}, bf16[1,2048,256]{2,1,0:T(8,128)(2,1)}, u32[]{:S(2)}) copy-start(bf16[1,2048,256]{2,1,0:T(8,128)(2,1)} %param.27) | copy-start | bytes 3145732
  179.4 1.3 copy-start.11
  180.7 1.3 copy-start.2
  185.2 7.4 %copy-start.12 = (bf16[2048,8]{0,1:T(8,128)(2,1)S(1)}, bf16[2048,8]{0,1:T(8,128)(2,1)}, u32[]{:S(2)}) copy-start(bf16[2048,8]{0,1:T(8,128)(2,1)} %param.26) | copy-start | bytes 98308
  185.2 103.9 %all-to-all-start.4 = ((bf16[128,8,2048]{2,1,0:T(8,128)(2,1)}), bf16[128,8,2048]{2,1,0:T(8,128)(2,1)}, u32[]{:S(2)}, u32[]{:S(2)}) async-start(bf16[128,8,2048]{2,1,0:T(8,128)(2,1)} %convert_bitcast_fusion), calls=%async_computation.4 | async-start | bytes 8388608 | tf_op jit(solution)/shard_map/all_to_all | solution.py:54
  193.5 101.4 %copy-start.6 = (f32[1,16,112]{2,1,0:T(8,128)S(1)}, f32[1,16,112]{2,1,0:T(8,128)}, u32[]{:S(2)}) copy-start(f32[1,16,112]{2,1,0:T(8,128)} %param.33) | copy-start | bytes 21508
  294.9 61.6 %copy-start.3 = (bf16[16,2048]{1,0:T(8,128)(2,1)}, bf16[16,2048]{1,0:T(8,128)(2,1)S(1)}, u32[]{:S(2)}) copy-start(bf16[16,2048]{1,0:T(8,128)(2,1)S(1)} %fusion.54) | copy-start | bytes 196612

commit v7 on v6

--- a/solution.py
+++ b/solution.py
@@ -190,7 +190,7 @@
     local_grad = jnp.einsum(
         "td,to->do", block_final, usage_grad, preferred_element_type=jnp.bfloat16
     )
-    head_total = a2a_allreduce(local_grad, ("ctx", "exp", "rep"), jnp.bfloat16).T
+    head_total = a2a_allreduce(local_grad, ("exp", "ctx", "rep"), jnp.bfloat16).T
     return (block_final[None], head_total)
 
 

time: 358 us -> 358 us (level)
  no operation moved by 1% of the time
where the time goes in v7:
time: 358 us; the launch traced here: 357 us
  blocking collectives  172 us (48%)
  waiting for transfers between devices  113 us (32%)
  matrix products  25.7 us (7%)
  starting transfers between devices  23.6 us (7%)
  other arithmetic  11.6 us (3%)
  local copies, waits for them, and re-layouts  11 us (3%)
    all_to_all x1, blocking collectives, token_move(): lax.all_to_all(blocks, ('ctx', 'exp'), split_axis=0, concat_axis=0, tiled...  104 us
    all_to_all x1, waiting for transfers between devices, token_move(): lax.all_to_all(blocks, ('ctx', 'exp'), split_axis=0, concat_axis=0, tiled...  94.8 us
    all_to_all x1, blocking collectives, a2a_reduce(): pieces = lax.all_to_all(sent, axes, 0, 0, tiled=True)  28.1 us
    all_to_all x1, blocking collectives, a2a_allreduce(): gathered = lax.all_to_all(spread, axes, 0, 0, tiled=True)  27 us
    all_to_all x1, blocking collectives, causal_convolve(): lax.all_to_all(convolved, 'ctx', split_axis=1, concat_axis=0, tiled=True)  12.6 us
    all_to_all x1, starting transfers between devices, causal_convolve(): whole = lax.all_to_all(both, 'ctx', split_axis=1, concat_axis=2, tiled=True)  10.1 us
    all_to_all x1, waiting for transfers between devices, a2a_reduce(): pieces = lax.all_to_all(sent, axes, 0, 0, tiled=True)  9.42 us
    all_to_all x1, waiting for transfers between devices, causal_convolve(): whole = lax.all_to_all(both, 'ctx', split_axis=1, concat_axis=2, tiled=True)  8.63 us
  transfers between devices with their start and end apart: 3, of which 3 were waited for; matrix products, arithmetic and copies ran while one was open for 1% of the time, Pallas kernels for 0%

profile of v7, /device:TPU:1, one launch (start us, length us, event | category | flops | bytes accessed | tf_op | source)
XLA Modules:
  0.0 357.5 jit_solution(10891186501835801958)
XLA Ops:
  0.7 1.4 fusion.22
  2.7 1.7 fusion.35
  6.2 10.1 %all-to-all-start = ((f32[2,256,128]{2,0,1:T(2,128)}), f32[2,256,128]{2,0,1:T(2,128)S(1)}, u32[]{:S(2)}, u32[]{:S(2)}) async-start(f32[2,256,128]{2,0,1:T(2,128)} %copy.30), calls=%async_computation | async-start | bytes 524288 | tf_op jit(solution)/shard_map/all_to_all | solution.py:102
  16.4 8.6 %all-to-all-done = f32[2,256,128]{2,0,1:T(2,128)S(1)} async-done(((f32[2,256,128]{2,0,1:T(2,128)}), f32[2,256,128]{2,0,1:T(2,128)S(1)}, u32[]{:S(2)}, u32[]{:S(2)}) %all-to-all-start) | async-done | bytes 262176 | tf_op jit(solution)/shard_map/all_to_all | solution.py:102
  26.1 2.1 fusion.90
  28.3 2.1 convolution_negate_fusion
  32.7 1.1 convolution_subtract_fusion
  40.8 12.6 %all_to_all.56 = f32[16,16,128]{2,0,1:T(8,128)S(1)} all-to-all(f32[16,16,128]{2,0,1:T(8,128)S(1)} %copy.33), channel_id=1, replica_groups=mesh['ctx'=16,'exp'=8,'rep'=2] {'ctx'}, dimensions={1} | all-to-all | bytes 262144 | tf_op jit(solution)/shard_map/all_to_all | solution.py:104
  53.6 2.5 convolution_convert_fusion
  56.1 6.8 %all-to-all-start.2 = ((bf16[8,16,2048]{2,1,0:T(8,128)(2,1)}), bf16[8,16,2048]{2,1,0:T(8,128)(2,1)}, u32[]{:S(2)}, u32[]{:S(2)}) async-start(bf16[8,16,2048]{2,1,0:T(8,128)(2,1)} %bitcast.168), calls=%async_computation.2 | async-start | bytes 1048576 | tf_op jit(solution)/shard_map/all_to_all | solution.py:37
  63.0 9.4 %all-to-all-done.2 = bf16[8,16,2048]{2,1,0:T(8,128)(2,1)} async-done(((bf16[8,16,2048]{2,1,0:T(8,128)(2,1)}), bf16[8,16,2048]{2,1,0:T(8,128)(2,1)}, u32[]{:S(2)}, u32[]{:S(2)}) %all-to-all-start.2) | async-done | bytes 524320 | tf_op jit(solution)/shard_map/all_to_all | solution.py:37
  75.4 104.0 %all_to_all.57 = bf16[128,8,2048]{2,1,0:T(8,128)(2,1)S(1)} all-to-all(bf16[128,8,2048]{2,1,0:T(8,128)(2,1)S(1)} %bitcast.165), channel_id=1, replica_groups=mesh['ctx'=16,'exp'=8,'rep'=2] {'ctx','exp'}, dimensions={0} | all-to-all | bytes 8388608 | tf_op jit(solution)/shard_map/all_to_all | solution.py:54
  179.4 1.3 fusion.2
  180.7 1.3 fusion.8
  182.0 3.2 convert_bitcast_fusion
  185.2 6.7 %all-to-all-start.4 = ((bf16[128,8,2048]{2,1,0:T(8,128)(2,1)}), bf16[128,8,2048]{2,1,0:T(8,128)(2,1)}, u32[]{:S(2)}, u32[]{:S(2)}) async-start(bf16[128,8,2048]{2,1,0:T(8,128)(2,1)} %convert_bitcast_fusion), calls=%async_computation.4 | async-start | bytes 8388608 | tf_op jit(solution)/shard_map/all_to_all | solution.py:54
  194.3 94.8 %all-to-all-done.4 = bf16[128,8,2048]{2,1,0:T(8,128)(2,1)} async-done(((bf16[128,8,2048]{2,1,0:T(8,128)(2,1)}), bf16[128,8,2048]{2,1,0:T(8,128)(2,1)}, u32[]{:S(2)}, u32[]{:S(2)}) %all-to-all-start.4) | async-done | bytes 4194336 | tf_op jit(solution)/shard_map/all_to_all | solution.py:54
  289.1 3.0 reduce_sum.64
  292.7 1.2 gather_fusion.1
  294.9 2.6 convolution_bitcast_fusion
  297.5 28.1 %all_to_all.58 = bf16[256,8,112]{2,1,0:T(8,128)(2,1)} all-to-all(bf16[256,8,112]{2,1,0:T(8,128)(2,1)} %convolution_bitcast_fusion), channel_id=1, replica_groups=mesh['ctx'=16,'exp'=8,'rep'=2] {'exp','ctx','rep'}, dimensions={0} | all-to-all | bytes 917504 | tf_op jit(solution)/shard_map/all_to_all | solution.py:37
  325.6 1.3 reduce_sum.65
  327.0 27.0 %all_to_all.59 = bf16[256,8,112]{2,1,0:T(8,128)(2,1)S(1)} all-to-all(bf16[256,8,112]{2,1,0:T(8,128)(2,1)S(1)} %broadcast_in_dim.21), channel_id=1, replica_groups=mesh['ctx'=16,'exp'=8,'rep'=2] {'exp','ctx','rep'}, dimensions={0} | all-to-all | bytes 917504 | tf_op jit(solution)/shard_map/all_to_all | solution.py:49
  355.0 2.5 copy.38
  (74 shorter events, 20.9 us)
Async XLA Ops:
  0.6 2.1 copy-start
  0.6 4.5 %copy-start.4 = (f32[128,256]{1,0:T(8,128)S(1)}, f32[128,256]{1,0:T(8,128)}, u32[]{:S(2)}) copy-start(f32[128,256]{1,0:T(8,128)} %param.21) | copy-start | bytes 393220
  4.4 0.7 copy-start.1
  6.2 18.9 %all-to-all-start = ((f32[2,256,128]{2,0,1:T(2,128)}), f32[2,256,128]{2,0,1:T(2,128)S(1)}, u32[]{:S(2)}, u32[]{:S(2)}) async-start(f32[2,256,128]{2,0,1:T(2,128)} %copy.30), calls=%async_computation | async-start | bytes 524288 | tf_op jit(solution)/shard_map/all_to_all | solution.py:102
  35.9 17.6 %copy-start.8 = (f32[256]{0:T(256)S(1)}, f32[256]{0:T(256)}, u32[]{:S(2)}) copy-start(f32[256]{0:T(256)} %param.23) | copy-start | bytes 3076
  37.3 25.6 %copy-start.5 = (s32[1,16,2]{1,2,0:T(2,128)S(1)}, s32[1,16,2]{1,2,0:T(2,128)}, u32[]{:S(2)}) copy-start(s32[1,16,2]{1,2,0:T(2,128)} %param.30) | copy-start | bytes 388
  37.4 25.6 %copy-start.9 = (s32[1,16,2]{1,2,0:T(2,128)S(1)}, s32[1,16,2]{1,2,0:T(2,128)}, u32[]{:S(2)}) copy-start(s32[1,16,2]{1,2,0:T(2,128)} %param.31) | copy-start | bytes 388
  38.1 36.5 %copy-start.7 = (f32[2048]{0:T(1024)S(1)}, f32[2048]{0:T(1024)}, u32[]{:S(2)}) copy-start(f32[2048]{0:T(1024)} %param.25) | copy-start | bytes 24580
  56.1 16.3 %all-to-all-start.2 = ((bf16[8,16,2048]{2,1,0:T(8,128)(2,1)}), bf16[8,16,2048]{2,1,0:T(8,128)(2,1)}, u32[]{:S(2)}, u32[]{:S(2)}) async-start(bf16[8,16,2048]{2,1,0:T(8,128)(2,1)} %bitcast.168), calls=%async_computation.2 | async-start | bytes 1048576 | tf_op jit(solution)/shard_map/all_to_all | solution.py:37
  75.3 104.0 %copy-start.10 = (bf16[1,2048,256]{2,1,0:T(8,128)(2,1)S(1)}, bf16[1,2048,256]{2,1,0:T(8,128)(2,1)}, u32[]{:S(2)}) copy-start(bf16[1,2048,256]{2,1,0:T(8,128)(2,1)} %param.27) | copy-start | bytes 3145732
  179.4 1.3 copy-start.11
  180.7 1.3 copy-start.2
  185.2 7.4 %copy-start.12 = (bf16[2048,8]{0,1:T(8,128)(2,1)S(1)}, bf16[2048,8]{0,1:T(8,128)(2,1)}, u32[]{:S(2)}) copy-start(bf16[2048,8]{0,1:T(8,128)(2,1)} %param.26) | copy-start | bytes 98308
  185.2 103.9 %all-to-all-start.4 = ((bf16[128,8,2048]{2,1,0:T(8,128)(2,1)}), bf16[128,8,2048]{2,1,0:T(8,128)(2,1)}, u32[]{:S(2)}, u32[]{:S(2)}) async-start(bf16[128,8,2048]{2,1,0:T(8,128)(2,1)} %convert_bitcast_fusion), calls=%async_computation.4 | async-start | bytes 8388608 | tf_op jit(solution)/shard_map/all_to_all | solution.py:54
  193.5 101.4 %copy-start.6 = (f32[1,16,112]{2,1,0:T(8,128)S(1)}, f32[1,16,112]{2,1,0:T(8,128)}, u32[]{:S(2)}) copy-start(f32[1,16,112]{2,1,0:T(8,128)} %param.33) | copy-start | bytes 21508
  294.9 62.5 %copy-start.3 = (bf16[16,2048]{1,0:T(8,128)(2,1)}, bf16[16,2048]{1,0:T(8,128)(2,1)S(1)}, u32[]{:S(2)}) copy-start(bf16[16,2048]{1,0:T(8,128)(2,1)S(1)} %fusion.54) | copy-start | bytes 196612
